TPU v7x, 128 devices: a whole 4x4x4 slice. The times are simulated.
128 devices in a mesh: lead: 32 (over x, y_lo, z), sub: 4 (over y_hi, core).
Axes of the slice: x: 4, y: 4 (y_hi: 2, y_lo: 2; y = y_hi * 2 + y_lo), z: 4, core: 2. Of those that a mesh axis runs over, the one named last changes fastest.
Arguments:
- state: float32 [67108864], P(('lead', 'sub')), may hold values from 0.135 to 67, as said below
- couplings: float32 [2, 16], replicated, may hold values from 0.25 to 16, as said below
Outputs:
- evolved: float32 [67108864], P(('lead', 'sub'))
- log_growth: float32 [], replicated
Inputs may be any that keep to these rules, and one draw needn't show every extreme that they name: `state`: every entry is positive. `couplings`: row 0 lies between 8 and 16, row 1 between 0.25 and 0.5.
All inputs are finite; a program needn't handle non-finite values.
Results may differ from a plain program's by a relative error of at most 0.0003.
Values sent between devices are 32-bit elements; how exact they have to be, the bound alone decides.
No kernel may reach another device: no remote copies, remote signals or barrier semaphores. Data moves between devices by JAX's collectives and lax.ppermute only.
A program may use at most 64 MiB of HBM per device.

v0:
```python
import jax
import jax.numpy as jnp
from jax import lax
from jax.sharding import PartitionSpec as P

BLOCK = 4
WINDOWS = 2
AXES = ("lead", "sub")
LANES = 128


def block_kernel(vertical, horizontal, spread):
    position = jnp.arange(spread, dtype=jnp.int32)
    digits = [position // 4 ** (BLOCK - 1 - level) % 4 for level in range(BLOCK)]
    kernel = jnp.ones((spread, spread), jnp.float32)
    for level in range(BLOCK):
        same_spin = (digits[level][:, None] == digits[level][None, :]).astype(jnp.float32)
        kernel = kernel * (1.0 + vertical[level] * same_spin)
    for level in range(1, BLOCK):
        chained = (digits[level - 1] == digits[level]).astype(jnp.float32)
        kernel = kernel * (1.0 + horizontal[level] * chained)[None, :]
    labels = jnp.arange(4, dtype=jnp.int32)
    first_bond = 1.0 + horizontal[0] * (labels[:, None] == labels[None, :]).astype(jnp.float32)
    return (kernel, first_bond)


def dot(lhs, rhs, lhs_dims, rhs_dims):
    return lax.dot_general(
        lhs,
        rhs,
        ((lhs_dims, rhs_dims), ((), ())),
        precision=lax.Precision.HIGHEST,
        preferred_element_type=jnp.float32,
    )


def exchange(rows):
    devices = rows.shape[0]
    shaped = rows.reshape(devices, -1, LANES)
    return lax.all_to_all(shaped, AXES, 0, 0, tiled=True).reshape(devices, -1)


def shards(state, couplings):
    lead_count = lax.axis_size("lead")
    sub_count = lax.axis_size("sub")
    devices = lead_count * sub_count
    me = lax.axis_index("lead") * sub_count + lax.axis_index("sub")
    spread = 4**BLOCK
    quarter = spread // 4
    whole_count = state.shape[0] * devices
    kernels = []
    for block in range(2 * WINDOWS):
        first_site = block * BLOCK
        kernels.append(
            block_kernel(
                couplings[0, first_site : first_site + BLOCK],
                couplings[1, first_site : first_site + BLOCK],
                spread,
            )
        )
    (kernel1, bond1), (kernel2, bond2), (kernel3, bond3), (kernel4, bond4) = kernels
    column = jnp.arange(spread, dtype=jnp.int32)

    received = exchange(state.reshape(-1, LANES).T)
    kernel1 = kernel1 * bond1[me % 4, column // quarter][None, :]
    current = dot(received.reshape(spread, -1), kernel1, (0,), (0,))
    current = dot(current.reshape(spread, -1, spread), kernel2, (0,), (0,))
    pattern2 = bond2[column % 4][:, column // quarter]
    current = current * pattern2[None, :, :]

    tail = kernel4.reshape(spread, 4, quarter).sum(axis=2)
    tail = dot(tail, bond4, (1,), (1,))
    gather = bond3[:, column // quarter].T[:, None, :] * tail[:, column % 4].T[:, :, None]
    per = spread // (devices // 4)
    rows = lax.dynamic_slice_in_dim(kernel3.reshape(per, devices // 4, spread), me // 4, 1, axis=1)
    cols = lax.dynamic_slice_in_dim(gather, (me % 4) * quarter, quarter, axis=1)
    weight = dot(rows.reshape(per, spread), cols.reshape(spread, -1), (1,), (0,))
    weight = weight.reshape(per, quarter, 1, 4)
    selector = (column[:, None] % 4 == jnp.arange(4)[None, :]).astype(jnp.float32)
    marginal = dot(current.reshape(-1, spread), selector, (1,), (0,))
    middle_part = jnp.sum(marginal)
    final_part = jnp.sum(marginal.reshape(per, quarter, 4, 4) * weight)

    sending = current.reshape(per * quarter, -1).T.reshape(devices, -1)
    extra = jnp.zeros((devices, LANES), jnp.float32)
    extra = extra.at[:, 0].set(middle_part).at[:, 1].set(final_part)
    received = exchange(jnp.concatenate([sending, extra], axis=1))
    middle_total = jnp.sum(received[:, -LANES])
    final_total = jnp.sum(received[:, -LANES + 1])
    current = received[:, :-LANES].reshape(devices // 4, 4, 8, per, quarter)
    kernel3 = kernel3.reshape(per, devices // 4, spread).transpose(1, 0, 2)
    current = dot(current, kernel3, (0, 3), (0, 1))
    pattern3 = bond3[jnp.arange(8) % 4][:, column // quarter]
    current = current * pattern3[None, :, None, :]
    current = dot(current, kernel4.reshape(4, quarter, spread), (0, 2), (0, 1))
    pattern4 = bond4[column % 4][:, column // quarter]

    middle_mean = middle_total / whole_count
    last_mean = final_total / middle_mean / whole_count
    current = current * pattern4[None, :, :] / (middle_mean * last_mean)
    growth = jnp.log(middle_mean) + jnp.log(last_mean)
    return (current.reshape(-1), growth)


def solution(mesh):
    in_specs = (P(AXES), P())
    out_specs = (P(AXES), P())
    return jax.shard_map(shards, mesh=mesh, in_specs=in_specs, out_specs=out_specs, check_vma=False)
```

profile of v0, /device:TPU:1, one launch (start us, length us, event | category | flops | bytes accessed | tf_op | source)
XLA Modules:
  0.0 159.2 jit_solution(5446591545447250664)
XLA Ops:
  0.6 3.0 %copy.62 = f32[128,32,128]{2,1,0:T(8,128)} copy(f32[128,32,128]{0,2,1:T(8,128)} %bitcast.96) | data formatting | bytes 4194304 | tf_op jit(solution)/shard_map/reshape | solution.py:39
  3.7 11.5 %all-to-all-start = ((f32[128,32,128]{2,1,0:T(8,128)}), f32[128,32,128]{2,1,0:T(8,128)S(1)}, u32[]{:S(2)}, u32[]{:S(2)}) async-start(f32[128,32,128]{2,1,0:T(8,128)} %copy.62), calls=%async_computation | async-start | bytes 4194304 | tf_op jit(solution)/shard_map/all_to_all | solution.py:40
  18.0 1.3 select_add_fusion.3
  19.3 2.9 %multiply_reduce_fusion = f32[256,4]{0,1:T(4,128)S(1)} fusion(f32[4,64]{1,0:T(4,128)S(1)} %get-tuple-element.68, f32[4,64]{1,0:T(4,128)S(1)} %get-tuple-element.69, f32[4,64]{1,0:T(4,128)S(1)} %select_add_fusion.5, f32[]{:T(128)} %bitcast.42, s32[4,64]{1,0:T(4,128)S(1)} %get-tuple-element.64, s32[256]{0:T(256)S(1)} %get-tuple-element.70, f32[]{:T(128)} %bitcast.41, ...), kind=kLoop, calls=%fused_computation.83 | loop fusion | flops 1244160 | bytes 15376 | tf_op jit(solution)/shard_map/reduce_sum | solution.py:71
  25.6 1.2 select_add_fusion.11
  26.9 1.4 select_add_fusion.13
  35.5 2.4 %gather_fusion = f32[256]{0:T(256)S(1)} fusion(f32[4,4]{1,0:T(4,128)S(1)} %select_add_fusion.8, s32[256]{0:T(256)S(1)} %bitcast.90), kind=kCustom, calls=%fused_computation | custom fusion | bytes 4096 | tf_op jit(solution)/shard_map/gather | solution.py:65
  40.5 1.3 select_add_fusion.18
  41.8 1.2 select_add_fusion.15
  43.0 1.7 %all-to-all-done = f32[128,32,128]{2,1,0:T(8,128)S(1)} async-done(((f32[128,32,128]{2,1,0:T(8,128)}), f32[128,32,128]{2,1,0:T(8,128)S(1)}, u32[]{:S(2)}, u32[]{:S(2)}) %all-to-all-start) | async-done | bytes 2097184 | tf_op jit(solution)/shard_map/all_to_all | solution.py:40
  44.7 1.5 reshape_reshape.3
  46.2 6.1 %convolution_bitcast_fusion = f32[2048,256]{0,1:T(8,128)S(1)} fusion(f32[256,2048]{1,0:T(8,128)} %reshape_reshape.3, f32[256]{0:T(256)S(1)} %gather_fusion, f32[256]{0:T(256)S(1)} %get-tuple-element.82, f32[256]{0:T(256)S(1)} %get-tuple-element.83, f32[256]{0:T(256)S(1)} %select_add_fusion.20, f32[]{:T(128)} %bitcast.3, s32[256]{0:T(256)S(1)} %get-tuple-element.70, ...), kind=kOutput, calls=%fused_computation.11 | convolution fusion | flops 1611857920 | bytes 4202512 | tf_op jit(solution)/shard_map/dot_general | solution.py:28
  52.3 1.8 %copy.63 = f32[2048,256]{1,0:T(8,128)} copy(f32[2048,256]{0,1:T(8,128)S(1)} %convolution_bitcast_fusion) | data formatting | bytes 4194304 | tf_op jit(solution)/shard_map/dot_general | solution.py:28
  54.1 8.0 %fusion.6 = f32[8,256,256]{2,1,0:T(8,128)S(1)} fusion(f32[256,8,256]{2,1,0:T(8,128)} %bitcast.94, f32[256,256]{1,0:T(8,128)S(1)} %copy.66, f32[256]{0:T(256)S(1)} %get-tuple-element.80, f32[256]{0:T(256)S(1)} %get-tuple-element.81, f32[256]{0:T(256)S(1)} %select_add_fusion.17, f32[]{:T(128)} %bitcast.17, f32[]{:T(128)} %bitcast.16, f32[]{:T(128)} %bitcast.15, ...), kind=kOutput, calls=%fused_computation.19 | convolution fusion | flops 1612316672 | bytes 4463632 | tf_op jit(solution)/shard_map/dot_general | solution.py:28
  62.1 1.6 %reshape.709 = f32[512,1024]{1,0:T(8,128)} reshape(f32[8,256,256]{2,1,0:T(8,128)S(1)} %fusion.6) | data formatting | bytes 4194304 | tf_op jit(solution)/shard_map/reshape | solution.py:84
  63.8 2.9 %copy.67 = f32[512,1024]{0,1:T(8,128)} copy(f32[512,1024]{1,0:T(8,128)} %reshape.709) | data formatting | bytes 4194304 | tf_op jit(solution)/shard_map/reshape | solution.py:84
  66.7 2.7 %reshape.710 = f32[128,4096]{1,0:T(8,128)} reshape(f32[1024,512]{1,0:T(8,128)} %bitcast.95) | data formatting | bytes 4194304 | tf_op jit(solution)/shard_map/reshape | solution.py:84
  69.4 1.7 %multiply_reduce_fusion.1 = (f32[]{:T(128)}, f32[]{:T(128)}) fusion(f32[2048,4]{0,1:T(4,128)S(1)} %mul.605, f32[2048,256]{1,0:T(8,128)S(1)} %bitcast.89, s32[256]{0:T(256)S(1)} %get-tuple-element.70), kind=kOutput, calls=%fused_computation.169 | convolution fusion | flops 25191422 | bytes 2130952 | tf_op jit(solution)/shard_map/dot_general | solution.py:28
  74.1 1.7 %pad_maximum_fusion = f32[128,4224]{1,0:T(8,128)S(1)} fusion(f32[128,128]{1,0:T(8,128)S(1)} %scatter.14, f32[128,4096]{1,0:T(8,128)} %reshape.710), kind=kLoop, calls=%fused_computation.12 | loop fusion | flops 540672 | bytes 4325376 | tf_op jit(solution)/shard_map/concatenate | solution.py:87
  75.9 2.0 %copy.72 = f32[128,4224]{0,1:T(8,128)} copy(f32[128,4224]{1,0:T(8,128)S(1)} %pad_maximum_fusion) | data formatting | bytes 4325376 | tf_op jit(solution)/shard_map/concatenate | solution.py:87
  77.8 3.5 %copy.73 = f32[128,33,128]{2,1,0:T(8,128)} copy(f32[128,33,128]{0,2,1:T(8,128)} %bitcast.91) | data formatting | bytes 4325376 | tf_op jit(solution)/shard_map/reshape | solution.py:39
  81.3 8.1 %all-to-all-start.1 = ((f32[128,33,128]{2,1,0:T(8,128)}), f32[128,33,128]{2,1,0:T(8,128)S(1)}, u32[]{:S(2)}, u32[]{:S(2)}) async-start(f32[128,33,128]{2,1,0:T(8,128)} %copy.73), calls=%async_computation.1 | async-start | bytes 5242880 | tf_op jit(solution)/shard_map/all_to_all | solution.py:40
  93.4 1.3 select_add_fusion.9
  94.7 29.5 %all-to-all-done.1 = f32[128,33,128]{2,1,0:T(8,128)S(1)} async-done(((f32[128,33,128]{2,1,0:T(8,128)}), f32[128,33,128]{2,1,0:T(8,128)S(1)}, u32[]{:S(2)}, u32[]{:S(2)}) %all-to-all-start.1) | async-done | bytes 2162720 | tf_op jit(solution)/shard_map/all_to_all | solution.py:40
  124.3 2.0 %copy.74 = f32[128,33,128]{0,2,1:T(8,128)} copy(f32[128,33,128]{2,1,0:T(8,128)S(1)} %all-to-all-done.1) | data formatting | bytes 4325376 | tf_op jit(solution)/shard_map/all_to_all | solution.py:40
  126.3 1.4 slice_reduce_fusion
  129.7 3.0 %slice.259 = f32[128,4096]{0,1:T(8,128)} slice(f32[128,4224]{0,1:T(8,128)} %bitcast.93), slice={[0:128], [0:4096]} | slice | bytes 4194304 | tf_op jit(solution)/shard_map/slice | solution.py:90
  132.8 1.9 %copy.75 = f32[128,4096]{1,0:T(8,128)S(1)} copy(f32[128,4096]{0,1:T(8,128)} %slice.259) | data formatting | bytes 4194304 | tf_op jit(solution)/shard_map/slice | solution.py:90
  134.7 3.0 %reshape.718 = f32[32,4,8,8,64]{4,3,2,1,0:T(8,128)} reshape(f32[128,4096]{1,0:T(8,128)S(1)} %copy.75) | data formatting | bytes 4194304 | tf_op jit(solution)/shard_map/reshape | solution.py:90
  137.7 11.6 %fusion = f32[4,8,64,256,1]{3,2,4,0,1:T(8,128)S(1)} fusion(f32[32,4,8,8,64]{4,3,2,1,0:T(8,128)} %reshape.718, f32[256]{0:T(256)S(1)} %get-tuple-element.77, f32[256]{0:T(256)S(1)} %get-tuple-element.78, f32[256]{0:T(256)S(1)} %get-tuple-element.79, f32[]{:T(128)} %bitcast.32, s32[256]{0:T(256)S(1)} %get-tuple-element.70, s32[32,8]{1,0:T(8,128)S(1)} %get-tuple-element.84, ...), kind=kOutput, calls=%fused_computation.9 | convolution fusion | flops 1611792384 | bytes 4205584 | tf_op jit(solution)/shard_map/dot_general | solution.py:28
  149.4 6.3 %fusion.2 = f32[8,256,256]{2,1,0:T(8,128)S(1)} fusion(f32[4,8,64,256,1]{3,2,4,0,1:T(8,128)S(1)} %fusion, f32[]{:T(128)S(6)} %mul.652, f32[256,256]{1,0:T(8,128)S(1)} %copy.80, f32[8,256]{1,0:T(8,128)S(1)} %copy.78, f32[256]{0:T(256)S(1)} %get-tuple-element.74, f32[256]{0:T(256)S(1)} %get-tuple-element.75, f32[256]{0:T(256)S(1)} %get-tuple-element.76, ...), kind=kOutput, calls=%fused_computation.14 | convolution fusion | flops 1613365248 | bytes 4475924 | tf_op jit(solution)/shard_map/dot_general | solution.py:28
  155.7 2.4 %copy.83 = f32[256,2,8,128]{3,1,2,0:T(2,128)} copy(f32[256,2,8,128]{3,2,1,0:T(8,128)S(1)} %bitcast.97) | data formatting | bytes 4194304
  (62 shorter events, 20.3 us)
Async XLA Ops:
  3.7 11.5 %copy-start = (f32[2,16]{1,0:T(2,128)S(1)}, f32[2,16]{1,0:T(2,128)}, u32[]{:S(2)}) copy-start(f32[2,16]{1,0:T(2,128)} %param.7) | copy-start | bytes 388
  3.7 41.1 %all-to-all-start = ((f32[128,32,128]{2,1,0:T(8,128)}), f32[128,32,128]{2,1,0:T(8,128)S(1)}, u32[]{:S(2)}, u32[]{:S(2)}) async-start(f32[128,32,128]{2,1,0:T(8,128)} %copy.62), calls=%async_computation | async-start | bytes 4194304 | tf_op jit(solution)/shard_map/all_to_all | solution.py:40
  81.3 43.0 %all-to-all-start.1 = ((f32[128,33,128]{2,1,0:T(8,128)}), f32[128,33,128]{2,1,0:T(8,128)S(1)}, u32[]{:S(2)}, u32[]{:S(2)}) async-start(f32[128,33,128]{2,1,0:T(8,128)} %copy.73), calls=%async_computation.1 | async-start | bytes 5242880 | tf_op jit(solution)/shard_map/all_to_all | solution.py:40
where the time goes:
time: 160 us; the launch traced here: 159 us
  local copies, waits for them, and re-layouts  44.1 us (28%)
  matrix products  35.5 us (22%)
  waiting for transfers between devices  31.2 us (20%)
  other arithmetic  21.9 us (14%)
  starting transfers between devices  19.6 us (12%)
  between operations  6.81 us (4%)
    dot_general x7, matrix products, dot(): lax.dot_general(lhs, rhs, ((lhs_dims, rhs_dims), ((), ())), precision=lax...  35.5 us
    all_to_all x2, waiting for transfers between devices, exchange(): return lax.all_to_all(shaped, AXES, 0, 0, tiled=True).reshape(devices, -1)  31.2 us
    all_to_all x2, starting transfers between devices, exchange(): return lax.all_to_all(shaped, AXES, 0, 0, tiled=True).reshape(devices, -1)  19.6 us
    add x9, other arithmetic, block_kernel(): kernel = kernel * (1.0 + horizontal[level] * chained)[None, :]  9.5 us
    reshape x3, local copies, waits for them, and re-layouts, shards(): sending = current.reshape(per * quarter, -1).T.reshape(devices, -1)  7.29 us
    reshape x2, local copies, waits for them, and re-layouts, exchange(): shaped = rows.reshape(devices, -1, LANES)  6.51 us
    slice x2, local copies, waits for them, and re-layouts, shards(): current = received[:, :-LANES].reshape(devices // 4, 4, 8, per, quarter)  4.97 us
  transfers between devices with their start and end apart: 2, of which 2 were waited for; matrix products, arithmetic and copies ran while one was open for 21% of the time, Pallas kernels for 0%

commit v1 on v0

--- a/solution.py
+++ b/solution.py
@@ -81,13 +81,15 @@
     middle_part = jnp.sum(marginal)
     final_part = jnp.sum(marginal.reshape(per, quarter, 4, 4) * weight)
 
-    sending = current.reshape(per * quarter, -1).T.reshape(devices, -1)
-    extra = jnp.zeros((devices, LANES), jnp.float32)
-    extra = extra.at[:, 0].set(middle_part).at[:, 1].set(final_part)
-    received = exchange(jnp.concatenate([sending, extra], axis=1))
-    middle_total = jnp.sum(received[:, -LANES])
-    final_total = jnp.sum(received[:, -LANES + 1])
-    current = received[:, :-LANES].reshape(devices // 4, 4, 8, per, quarter)
+    sending = current.reshape(per * quarter, -1).T.reshape(devices, -1, LANES)
+    lane = jnp.arange(LANES, dtype=jnp.int32)
+    extra = jnp.where(lane == 0, middle_part, jnp.where(lane == 1, final_part, 0.0))
+    extra = jnp.broadcast_to(extra[None, None, :], (devices, 1, LANES))
+    received = lax.all_to_all(jnp.concatenate([sending, extra], axis=1), AXES, 0, 0, tiled=True)
+    middle_total = jnp.sum(received[:, -1, 0])
+    final_total = jnp.sum(received[:, -1, 1])
+    received = received[:, :-1, :]
+    current = received.reshape(devices // 4, 4, 8, per, quarter)
     kernel3 = kernel3.reshape(per, devices // 4, spread).transpose(1, 0, 2)
     current = dot(current, kernel3, (0, 3), (0, 1))
     pattern3 = bond3[jnp.arange(8) % 4][:, column // quarter]

time: 160 us -> 146 us (0.912)
  local copies, waits for them, and re-layouts: 44.1 us -> 34.2 us
  between operations: 6.81 us -> 4.24 us
  waiting for transfers between devices: 31.2 us -> 32.9 us
  starting transfers between devices: 19.6 us -> 18 us
    all_to_all x0 -> x1, waiting for transfers between devices: none -> 29.6 us  [shards(): lax.all_to_all(jnp.concatenate([sending, extra], axis=1), AXES, 0, 0, til...]
    all_to_all x2 -> x1, waiting for transfers between devices: 31.2 us -> 3.31 us  [exchange(): return lax.all_to_all(shaped, AXES, 0, 0, tiled=True).reshape(devices, -1)]
    all_to_all x2 -> x1, starting transfers between devices: 19.6 us -> 11.5 us  [exchange(): return lax.all_to_all(shaped, AXES, 0, 0, tiled=True).reshape(devices, -1)]
    all_to_all x0 -> x1, starting transfers between devices: none -> 6.48 us  [shards(): lax.all_to_all(jnp.concatenate([sending, extra], axis=1), AXES, 0, 0, til...]
    reshape x2 -> x1, local copies, waits for them, and re-layouts: 6.51 us -> 3.04 us  [exchange(): shaped = rows.reshape(devices, -1, LANES)]
    slice x2 -> x1, local copies, waits for them, and re-layouts: 4.97 us -> 1.61 us  [shards(): received = received[:, :-1, :]]
    all_to_all x1 -> x0, local copies, waits for them, and re-layouts: 2.03 us -> none  [exchange(): return lax.all_to_all(shaped, AXES, 0, 0, tiled=True).reshape(devices, -1)]
    concatenate x1 -> x0, local copies, waits for them, and re-layouts: 1.95 us -> none  [shards(): received = exchange(jnp.concatenate([sending, extra], axis=1))]
where the time goes in v1:
time: 146 us
  matrix products  35.4 us (24%)
  local copies, waits for them, and re-layouts  34.2 us (23%)
  waiting for transfers between devices  32.9 us (23%)
  other arithmetic  20.9 us (14%)
  starting transfers between devices  18 us (12%)
  between operations  4.24 us (3%)
    dot_general x7, matrix products, dot(): lax.dot_general(lhs, rhs, ((lhs_dims, rhs_dims), ((), ())), precision=lax...  35.4 us
    all_to_all x1, waiting for transfers between devices, shards(): lax.all_to_all(jnp.concatenate([sending, extra], axis=1), AXES, 0, 0, til...  29.6 us
    all_to_all x1, starting transfers between devices, exchange(): return lax.all_to_all(shaped, AXES, 0, 0, tiled=True).reshape(devices, -1)  11.5 us
    add x9, other arithmetic, block_kernel(): kernel = kernel * (1.0 + horizontal[level] * chained)[None, :]  9.22 us
    reshape x3, local copies, waits for them, and re-layouts, shards(): sending = current.reshape(per * quarter, -1).T.reshape(devices, -1, LANES)  7.17 us
    all_to_all x1, starting transfers between devices, shards(): lax.all_to_all(jnp.concatenate([sending, extra], axis=1), AXES, 0, 0, til...  6.48 us
    reshape x1, local copies, waits for them, and re-layouts, shards(): current = received.reshape(devices // 4, 4, 8, per, quarter)  4.33 us
    all_to_all x1, waiting for transfers between devices, exchange(): return lax.all_to_all(shaped, AXES, 0, 0, tiled=True).reshape(devices, -1)  3.31 us
  transfers between devices with their start and end apart: 2, of which 2 were waited for; matrix products, arithmetic and copies ran while one was open for 21% of the time, Pallas kernels for 0%

profile of v1, /device:TPU:1, one launch (start us, length us, event | category | flops | bytes accessed | tf_op | source)
XLA Modules:
  0.0 145.5 jit_solution(12254396405498998051)
XLA Ops:
  0.6 3.0 %copy.54 = f32[128,32,128]{2,1,0:T(8,128)} copy(f32[128,32,128]{0,2,1:T(8,128)} %bitcast.90) | data formatting | bytes 4194304 | tf_op jit(solution)/shard_map/reshape | solution.py:39
  3.7 11.5 %all-to-all-start = ((f32[128,32,128]{2,1,0:T(8,128)}), f32[128,32,128]{2,1,0:T(8,128)S(1)}, u32[]{:S(2)}, u32[]{:S(2)}) async-start(f32[128,32,128]{2,1,0:T(8,128)} %copy.54), calls=%async_computation | async-start | bytes 4194304 | tf_op jit(solution)/shard_map/all_to_all | solution.py:40
  18.1 1.2 select_add_fusion.3
  19.3 2.7 %multiply_reduce_fusion = f32[256,4]{0,1:T(4,128)S(1)} fusion(f32[4,64]{1,0:T(4,128)S(1)} %get-tuple-element.44, f32[4,64]{1,0:T(4,128)S(1)} %get-tuple-element.45, f32[4,64]{1,0:T(4,128)S(1)} %select_add_fusion.5, f32[]{:T(128)} %bitcast.41, s32[4,64]{1,0:T(4,128)S(1)} %get-tuple-element.40, s32[256]{0:T(256)S(1)} %get-tuple-element.46, f32[]{:T(128)} %bitcast.40, ...), kind=kLoop, calls=%fused_computation.83 | loop fusion | flops 1244160 | bytes 15376 | tf_op jit(solution)/shard_map/reduce_sum | solution.py:71
  22.8 1.0 gather_fusion.4
  25.5 1.1 select_add_fusion.11
  26.7 1.4 select_add_fusion.13
  28.9 1.0 gather_fusion.2
  32.5 1.1 fusion.42
  35.3 2.4 %gather_fusion = f32[256]{0:T(256)S(1)} fusion(f32[4,4]{1,0:T(4,128)S(1)} %select_add_fusion.8, s32[256]{0:T(256)S(1)} %bitcast.87), kind=kCustom, calls=%fused_computation | custom fusion | bytes 4096 | tf_op jit(solution)/shard_map/gather | solution.py:65
  39.0 1.2 select_add_fusion.18
  40.2 1.2 select_add_fusion.15
  41.4 3.3 %all-to-all-done = f32[128,32,128]{2,1,0:T(8,128)S(1)} async-done(((f32[128,32,128]{2,1,0:T(8,128)}), f32[128,32,128]{2,1,0:T(8,128)S(1)}, u32[]{:S(2)}, u32[]{:S(2)}) %all-to-all-start) | async-done | bytes 2097184 | tf_op jit(solution)/shard_map/all_to_all | solution.py:40
  44.7 1.5 %reshape_reshape.3 = f32[256,2048]{1,0:T(8,128)} reshape(f32[128,32,128]{2,1,0:T(8,128)S(1)} %all-to-all-done) | data formatting | bytes 4194304 | tf_op jit(solution)/shard_map/reshape;reshape | solution.py:66
  46.2 6.1 %convolution_bitcast_fusion = f32[2048,256]{0,1:T(8,128)S(1)} fusion(f32[256,2048]{1,0:T(8,128)} %reshape_reshape.3, f32[256]{0:T(256)S(1)} %gather_fusion, f32[256]{0:T(256)S(1)} %get-tuple-element.58, f32[256]{0:T(256)S(1)} %get-tuple-element.59, f32[256]{0:T(256)S(1)} %select_add_fusion.20, f32[]{:T(128)} %bitcast.3, s32[256]{0:T(256)S(1)} %get-tuple-element.46, ...), kind=kOutput, calls=%fused_computation.11 | convolution fusion | flops 1611857920 | bytes 4202512 | tf_op jit(solution)/shard_map/dot_general | solution.py:28
  52.3 1.8 %copy.55 = f32[2048,256]{1,0:T(8,128)} copy(f32[2048,256]{0,1:T(8,128)S(1)} %convolution_bitcast_fusion) | data formatting | bytes 4194304 | tf_op jit(solution)/shard_map/dot_general | solution.py:28
  54.1 7.9 %fusion.6 = f32[8,256,256]{2,1,0:T(8,128)S(1)} fusion(f32[256,8,256]{2,1,0:T(8,128)} %bitcast.88, f32[256,256]{1,0:T(8,128)S(1)} %copy.58, f32[256]{0:T(256)S(1)} %get-tuple-element.56, f32[256]{0:T(256)S(1)} %get-tuple-element.57, f32[256]{0:T(256)S(1)} %select_add_fusion.17, f32[]{:T(128)} %bitcast.17, f32[]{:T(128)} %bitcast.16, f32[]{:T(128)} %bitcast.15, ...), kind=kOutput, calls=%fused_computation.19 | convolution fusion | flops 1612316672 | bytes 4463632 | tf_op jit(solution)/shard_map/dot_general | solution.py:28
  62.0 1.6 %reshape.667 = f32[512,1024]{1,0:T(8,128)} reshape(f32[8,256,256]{2,1,0:T(8,128)S(1)} %fusion.6) | data formatting | bytes 4194304 | tf_op jit(solution)/shard_map/reshape | solution.py:84
  63.7 2.9 %copy.59 = f32[512,1024]{0,1:T(8,128)} copy(f32[512,1024]{1,0:T(8,128)} %reshape.667) | data formatting | bytes 4194304 | tf_op jit(solution)/shard_map/reshape | solution.py:84
  66.6 2.6 %reshape.668 = f32[128,32,128]{2,1,0:T(8,128)} reshape(f32[1024,512]{1,0:T(8,128)} %bitcast.89) | data formatting | bytes 4194304 | tf_op jit(solution)/shard_map/reshape | solution.py:84
  69.2 1.8 %fusion.218 = (f32[]{:T(128)}, f32[]{:T(128)}) fusion(f32[2048,4]{0,1:T(4,128)S(1)} %mul.605, f32[2048,256]{1,0:T(8,128)S(1)} %bitcast.86, s32[256]{0:T(256)S(1)} %get-tuple-element.46), kind=kOutput, calls=%fused_computation.347 | convolution fusion | flops 25191422 | bytes 2130952 | tf_op jit(solution)/shard_map/dot_general | solution.py:28
  71.0 1.3 compare_select_fusion.19
  72.3 1.7 %pad_maximum_fusion = f32[128,33,128]{2,1,0:T(8,128)} fusion(f32[128,1,128]{2,1,0:T(1,128)S(1)} %broadcast_in_dim.14, f32[128,32,128]{2,1,0:T(8,128)S(1)} %copy-done), kind=kLoop, calls=%fused_computation.12 | loop fusion | flops 540672 | bytes 4325376 | tf_op jit(solution)/shard_map/concatenate | solution.py:88
  74.0 6.5 %all-to-all-start.1 = ((f32[128,33,128]{2,1,0:T(8,128)}), f32[128,33,128]{2,1,0:T(8,128)S(1)}, u32[]{:S(2)}, u32[]{:S(2)}) async-start(f32[128,33,128]{2,1,0:T(8,128)} %pad_maximum_fusion), calls=%async_computation.1 | async-start | bytes 5242880 | tf_op jit(solution)/shard_map/all_to_all | solution.py:88
  83.4 1.0 gather_fusion.8
  84.6 1.2 select_add_fusion.9
  85.9 29.6 %all-to-all-done.1 = f32[128,33,128]{2,1,0:T(8,128)S(1)} async-done(((f32[128,33,128]{2,1,0:T(8,128)}), f32[128,33,128]{2,1,0:T(8,128)S(1)}, u32[]{:S(2)}, u32[]{:S(2)}) %all-to-all-start.1) | async-done | bytes 2162720 | tf_op jit(solution)/shard_map/all_to_all | solution.py:88
  118.3 1.6 %slice.230 = f32[128,32,128]{2,1,0:T(8,128)} slice(f32[128,33,128]{2,1,0:T(8,128)S(1)} %all-to-all-done.1), slice={[0:128], [0:32], [0:128]} | slice | bytes 4194304 | tf_op jit(solution)/shard_map/slice | solution.py:91
  119.9 4.3 %reshape.673 = f32[32,4,8,8,64]{4,3,2,1,0:T(8,128)} reshape(f32[128,32,128]{2,1,0:T(8,128)} %slice.230) | data formatting | bytes 4194304 | tf_op jit(solution)/shard_map/reshape | solution.py:92
  124.2 11.6 %fusion = f32[4,8,64,256,1]{3,2,4,0,1:T(8,128)S(1)} fusion(f32[32,4,8,8,64]{4,3,2,1,0:T(8,128)} %reshape.673, f32[256]{0:T(256)S(1)} %get-tuple-element.53, f32[256]{0:T(256)S(1)} %get-tuple-element.54, f32[256]{0:T(256)S(1)} %get-tuple-element.55, f32[]{:T(128)} %bitcast.31, s32[256]{0:T(256)S(1)} %get-tuple-element.46, s32[32,8]{1,0:T(8,128)S(1)} %get-tuple-element.60, ...), kind=kOutput, calls=%fused_computation.9 | convolution fusion | flops 1611792384 | bytes 4205584 | tf_op jit(solution)/shard_map/dot_general | solution.py:28
  135.9 6.1 %fusion.2 = f32[8,256,256]{2,1,0:T(8,128)S(1)} fusion(f32[4,8,64,256,1]{3,2,4,0,1:T(8,128)S(1)} %fusion, f32[]{:T(128)S(6)} %mul.652, f32[256,256]{1,0:T(8,128)S(1)} %copy.68, f32[8,256]{1,0:T(8,128)S(1)} %copy.66, f32[256]{0:T(256)S(1)} %get-tuple-element.50, f32[256]{0:T(256)S(1)} %get-tuple-element.51, f32[256]{0:T(256)S(1)} %get-tuple-element.52, ...), kind=kOutput, calls=%fused_computation.14 | convolution fusion | flops 1613365248 | bytes 4475924 | tf_op jit(solution)/shard_map/dot_general | solution.py:28
  142.0 2.4 %copy.71 = f32[256,2,8,128]{3,1,2,0:T(2,128)} copy(f32[256,2,8,128]{3,2,1,0:T(8,128)S(1)} %bitcast.91) | data formatting | bytes 4194304
  (56 shorter events, 15.5 us)
Async XLA Ops:
  3.7 11.5 %copy-start.1 = (f32[2,16]{1,0:T(2,128)S(1)}, f32[2,16]{1,0:T(2,128)}, u32[]{:S(2)}) copy-start(f32[2,16]{1,0:T(2,128)} %param.3) | copy-start | bytes 388
  3.7 41.1 %all-to-all-start = ((f32[128,32,128]{2,1,0:T(8,128)}), f32[128,32,128]{2,1,0:T(8,128)S(1)}, u32[]{:S(2)}, u32[]{:S(2)}) async-start(f32[128,32,128]{2,1,0:T(8,128)} %copy.54), calls=%async_computation | async-start | bytes 4194304 | tf_op jit(solution)/shard_map/all_to_all | solution.py:40
  69.2 3.1 %copy-start = (f32[128,32,128]{2,1,0:T(8,128)S(1)}, f32[128,32,128]{2,1,0:T(8,128)}, u32[]{:S(2)}) copy-start(f32[128,32,128]{2,1,0:T(8,128)} %reshape.668) | copy-start | bytes 6291460
  74.0 41.4 %all-to-all-start.1 = ((f32[128,33,128]{2,1,0:T(8,128)}), f32[128,33,128]{2,1,0:T(8,128)S(1)}, u32[]{:S(2)}, u32[]{:S(2)}) async-start(f32[128,33,128]{2,1,0:T(8,128)} %pad_maximum_fusion), calls=%async_computation.1 | async-start | bytes 5242880 | tf_op jit(solution)/shard_map/all_to_all | solution.py:88

commit v2 on v1

--- a/solution.py
+++ b/solution.py
@@ -85,23 +85,29 @@
     lane = jnp.arange(LANES, dtype=jnp.int32)
     extra = jnp.where(lane == 0, middle_part, jnp.where(lane == 1, final_part, 0.0))
     extra = jnp.broadcast_to(extra[None, None, :], (devices, 1, LANES))
-    received = lax.all_to_all(jnp.concatenate([sending, extra], axis=1), AXES, 0, 0, tiled=True)
-    middle_total = jnp.sum(received[:, -1, 0])
-    final_total = jnp.sum(received[:, -1, 1])
-    received = received[:, :-1, :]
-    current = received.reshape(devices // 4, 4, 8, per, quarter)
+    half = sending.shape[1] // 2
+    first = lax.all_to_all(
+        jnp.concatenate([sending[:, :half], extra], axis=1), AXES, 0, 0, tiled=True
+    )
+    second = lax.all_to_all(sending[:, half:], AXES, 0, 0, tiled=True)
+    middle_total = jnp.sum(first[:, -1, 0])
+    final_total = jnp.sum(first[:, -1, 1])
     kernel3 = kernel3.reshape(per, devices // 4, spread).transpose(1, 0, 2)
-    current = dot(current, kernel3, (0, 3), (0, 1))
-    pattern3 = bond3[jnp.arange(8) % 4][:, column // quarter]
-    current = current * pattern3[None, :, None, :]
-    current = dot(current, kernel4.reshape(4, quarter, spread), (0, 2), (0, 1))
+    pattern3 = bond3[jnp.arange(4)][:, column // quarter]
     pattern4 = bond4[column % 4][:, column // quarter]
-
+    kernel4 = kernel4.reshape(4, quarter, spread)
     middle_mean = middle_total / whole_count
     last_mean = final_total / middle_mean / whole_count
-    current = current * pattern4[None, :, :] / (middle_mean * last_mean)
+    scale = 1.0 / (middle_mean * last_mean)
+    outputs = []
+    for received in (first[:, :-1], second):
+        current = received.reshape(devices // 4, 4, 4, per, quarter)
+        current = dot(current, kernel3, (0, 3), (0, 1))
+        current = current * pattern3[None, :, None, :]
+        current = dot(current, kernel4, (0, 2), (0, 1))
+        outputs.append(current * pattern4[None, :, :])
     growth = jnp.log(middle_mean) + jnp.log(last_mean)
-    return (current.reshape(-1), growth)
+    return ((jnp.concatenate(outputs, axis=0) * scale).reshape(-1), growth)
 
 
 def solution(mesh):

time: 146 us -> 147 us (level)
  waiting for transfers between devices: 32.9 us -> 17.7 us
  matrix products: 35.4 us -> 40.4 us
  starting transfers between devices: 18 us -> 22 us
  other arithmetic: 20.9 us -> 24.2 us
  local copies, waits for them, and re-layouts: 34.2 us -> 37.3 us
    all_to_all x1 -> x2, waiting for transfers between devices: 29.6 us -> 12.4 us  [the longest x1 6.52 us: shards(): lax.all_to_all(jnp.concatenate([sending[:, :half], extra], axis=1), AXES,...]
    dot_general x7 -> x9, matrix products: 35.4 us -> 40.4 us  [dot(): lax.dot_general(lhs, rhs, ((lhs_dims, rhs_dims), ((), ())), precision=lax...]
    all_to_all x1 -> x2, starting transfers between devices: 6.48 us -> 10.5 us  [the longest x1 5.59 us: shards(): lax.all_to_all(jnp.concatenate([sending[:, :half], extra], axis=1), AXES,...]
    reshape x1 -> x2, local copies, waits for them, and re-layouts: 4.33 us -> 0.67 us  [shards(): current = received.reshape(devices // 4, 4, 4, per, quarter)]
    slice x2 -> x3, local copies, waits for them, and re-layouts: 2.29 us -> 5.08 us  [the longest x1 3.05 us: shards(): sending[:, :half]]
    mul x2, local copies, waits for them, and re-layouts: 1.01 us -> 3.2 us  [shards(): final_part = jnp.sum(marginal.reshape(per, quarter, 4, 4) * weight)]
    all_to_all x1, waiting for transfers between devices: 3.31 us -> 5.29 us  [exchange(): return lax.all_to_all(shaped, AXES, 0, 0, tiled=True).reshape(devices, -1)]
  transfers between devices with their start and end apart: 2 -> 3, of which waited for: 2 -> 3; matrix products, arithmetic and copies ran while one was open for 21% -> 37% of each run, Pallas kernels for 0% -> 0%
where the time goes in v2:
time: 147 us; the launch traced here: 146 us
  matrix products  40.4 us (27%)
  local copies, waits for them, and re-layouts  37.3 us (25%)
  other arithmetic  24.2 us (16%)
  starting transfers between devices  22 us (15%)
  waiting for transfers between devices  17.7 us (12%)
  between operations  4.53 us (3%)
    dot_general x9, matrix products, dot(): lax.dot_general(lhs, rhs, ((lhs_dims, rhs_dims), ((), ())), precision=lax...  40.4 us
    all_to_all x1, starting transfers between devices, exchange(): return lax.all_to_all(shaped, AXES, 0, 0, tiled=True).reshape(devices, -1)  11.5 us
    add x9, other arithmetic, block_kernel(): kernel = kernel * (1.0 + horizontal[level] * chained)[None, :]  10 us
    reshape x3, local copies, waits for them, and re-layouts, shards(): sending = current.reshape(per * quarter, -1).T.reshape(devices, -1, LANES)  7.15 us
    all_to_all x1, waiting for transfers between devices, shards(): lax.all_to_all(jnp.concatenate([sending[:, :half], extra], axis=1), AXES,...  6.52 us
    all_to_all x1, waiting for transfers between devices, shards(): second = lax.all_to_all(sending[:, half:], AXES, 0, 0, tiled=True)  5.9 us
    all_to_all x1, starting transfers between devices, shards(): lax.all_to_all(jnp.concatenate([sending[:, :half], extra], axis=1), AXES,...  5.59 us
    all_to_all x1, waiting for transfers between devices, exchange(): return lax.all_to_all(shaped, AXES, 0, 0, tiled=True).reshape(devices, -1)  5.29 us
  transfers between devices with their start and end apart: 3, of which 3 were waited for; matrix products, arithmetic and copies ran while one was open for 37% of the time, Pallas kernels for 0%

profile of v2, /device:TPU:1, one launch (start us, length us, event | category | flops | bytes accessed | tf_op | source)
XLA Modules:
  0.0 146.1 jit_solution(16247494384422503009)
XLA Ops:
  0.6 3.0 %copy.55 = f32[128,32,128]{2,1,0:T(8,128)} copy(f32[128,32,128]{0,2,1:T(8,128)} %bitcast.104) | data formatting | bytes 4194304 | tf_op jit(solution)/shard_map/reshape | solution.py:39
  3.7 11.5 %all-to-all-start = ((f32[128,32,128]{2,1,0:T(8,128)}), f32[128,32,128]{2,1,0:T(8,128)S(1)}, u32[]{:S(2)}, u32[]{:S(2)}) async-start(f32[128,32,128]{2,1,0:T(8,128)} %copy.55), calls=%async_computation | async-start | bytes 4194304 | tf_op jit(solution)/shard_map/all_to_all | solution.py:40
  18.7 1.4 select_add_fusion.3
  20.1 2.8 %multiply_reduce_fusion = f32[256,4]{0,1:T(4,128)S(1)} fusion(f32[4,64]{1,0:T(4,128)S(1)} %get-tuple-element.46, f32[4,64]{1,0:T(4,128)S(1)} %get-tuple-element.47, f32[4,64]{1,0:T(4,128)S(1)} %select_add_fusion.5, f32[]{:T(128)} %bitcast.41, s32[4,64]{1,0:T(4,128)S(1)} %get-tuple-element.42, s32[256]{0:T(256)S(1)} %get-tuple-element.48, f32[]{:T(128)} %bitcast.40, ...), kind=kLoop, calls=%fused_computation.65 | loop fusion | flops 1244160 | bytes 15376 | tf_op jit(solution)/shard_map/reduce_sum | solution.py:71
  28.3 2.4 %gather_fusion = f32[256]{0:T(256)S(1)} fusion(f32[4,4]{1,0:T(4,128)S(1)} %select_add_fusion.8, s32[256]{0:T(256)S(1)} %bitcast.100), kind=kCustom, calls=%fused_computation | custom fusion | bytes 4096 | tf_op jit(solution)/shard_map/gather | solution.py:65
  32.1 1.8 %select_add_fusion.11 = (f32[256]{0:T(256)}, f32[256]{0:T(256)S(1)}) fusion(f32[]{:T(128)} %bitcast.42, f32[]{:T(128)} %bitcast.34), kind=kLoop, calls=%fused_computation.258 | loop fusion | flops 16128 | bytes 2056 | tf_op jit(solution)/shard_map/add | solution.py:21
  36.5 1.4 compare_select_fusion.8
  38.0 1.4 select_add_fusion
  39.4 5.3 %all-to-all-done = f32[128,32,128]{2,1,0:T(8,128)S(1)} async-done(((f32[128,32,128]{2,1,0:T(8,128)}), f32[128,32,128]{2,1,0:T(8,128)S(1)}, u32[]{:S(2)}, u32[]{:S(2)}) %all-to-all-start) | async-done | bytes 2097184 | tf_op jit(solution)/shard_map/all_to_all | solution.py:40
  44.7 1.5 %reshape_reshape.3 = f32[256,2048]{1,0:T(8,128)} reshape(f32[128,32,128]{2,1,0:T(8,128)S(1)} %all-to-all-done) | data formatting | bytes 4194304 | tf_op jit(solution)/shard_map/reshape;reshape | solution.py:66
  46.2 6.2 %convolution_bitcast_fusion = f32[2048,256]{0,1:T(8,128)S(1)} fusion(f32[256,2048]{1,0:T(8,128)} %reshape_reshape.3, f32[256]{0:T(256)S(1)} %gather_fusion, f32[256]{0:T(256)S(1)} %get-tuple-element.60, f32[256]{0:T(256)S(1)} %get-tuple-element.61, f32[256]{0:T(256)S(1)} %select_add_fusion.20, f32[]{:T(128)} %bitcast.3, s32[256]{0:T(256)S(1)} %get-tuple-element.48, ...), kind=kOutput, calls=%fused_computation.9 | convolution fusion | flops 1611857920 | bytes 4202512 | tf_op jit(solution)/shard_map/dot_general | solution.py:28
  52.4 1.8 %copy.56 = f32[2048,256]{1,0:T(8,128)} copy(f32[2048,256]{0,1:T(8,128)S(1)} %convolution_bitcast_fusion) | data formatting | bytes 4194304 | tf_op jit(solution)/shard_map/dot_general | solution.py:28
  54.2 7.9 %fusion.6 = f32[8,256,256]{2,1,0:T(8,128)S(1)} fusion(f32[256,8,256]{2,1,0:T(8,128)} %bitcast.101, f32[256,256]{1,0:T(8,128)S(1)} %copy.59, f32[256]{0:T(256)S(1)} %get-tuple-element.58, f32[256]{0:T(256)S(1)} %get-tuple-element.59, f32[256]{0:T(256)S(1)} %select_add_fusion.17, f32[]{:T(128)} %bitcast.17, f32[]{:T(128)} %bitcast.16, f32[]{:T(128)} %bitcast.15, ...), kind=kOutput, calls=%fused_computation.17 | convolution fusion | flops 1612316672 | bytes 4463632 | tf_op jit(solution)/shard_map/dot_general | solution.py:28
  62.1 1.6 %reshape.640 = f32[512,1024]{1,0:T(8,128)} reshape(f32[8,256,256]{2,1,0:T(8,128)S(1)} %fusion.6) | data formatting | bytes 4194304 | tf_op jit(solution)/shard_map/reshape | solution.py:84
  63.7 2.9 %copy.60 = f32[512,1024]{0,1:T(8,128)} copy(f32[512,1024]{1,0:T(8,128)} %reshape.640) | data formatting | bytes 4194304 | tf_op jit(solution)/shard_map/reshape | solution.py:84
  66.7 2.6 %reshape.641 = f32[128,32,128]{2,1,0:T(8,128)} reshape(f32[1024,512]{1,0:T(8,128)} %bitcast.103) | data formatting | bytes 4194304 | tf_op jit(solution)/shard_map/reshape | solution.py:84
  69.3 3.1 %fusion.167 = (f32[128,16,128]{2,1,0:T(8,128)}, f32[128,16,128]{2,1,0:T(8,128)}) fusion(f32[128,32,128]{2,1,0:T(8,128)} %reshape.641), kind=kLoop, calls=%fused_computation.289 | loop fusion | bytes 4194304 | tf_op jit(solution)/shard_map/slice | solution.py:90
  72.3 4.9 %all-to-all-start.2 = ((f32[128,16,128]{2,1,0:T(8,128)}), f32[128,16,128]{2,1,0:T(8,128)S(1)}, u32[]{:S(2)}, u32[]{:S(2)}) async-start(f32[128,16,128]{2,1,0:T(8,128)} %get-tuple-element.7), calls=%async_computation.2 | async-start | bytes 2097152 | tf_op jit(solution)/shard_map/all_to_all | solution.py:92
  81.0 1.8 %fusion.57 = f32[8,64,4]{1,0,2:T(8,128)S(1)} fusion(f32[64,4,256]{2,1,0:T(4,128)S(1)} %reshape.645, f32[8,32,256]{2,0,1:T(8,128)} %compare_select_fusion.8, s32[]{:T(128)S(6)} %select_n.683, f32[8,32,256]{2,0,1:T(8,128)} %select_add_fusion, f32[8,32,256]{2,0,1:T(8,128)S(1)} %select_add_fusion.1, pred[8,32,256]{2,0,1:T(8,128)(4,1)S(1)} %broadcast_compare_fusion, ...), kind=kOutput, calls=%fused_computation.61 | convolution fusion | flops 6309888 | bytes 300548 | tf_op jit(solution)/shard_map/dot_general | solution.py:28
  84.1 1.9 %mul.627 = f32[2048,4]{0,1:T(4,128)S(1)} reshape(f32[8,64,4,4]{2,1,0,3:T(8,128)} %mul.626) | data formatting | bytes 65536 | tf_op jit(solution)/shard_map/mul | solution.py:82
  86.0 1.8 %fusion.166 = (f32[]{:T(128)}, f32[]{:T(128)}) fusion(f32[2048,4]{0,1:T(4,128)S(1)} %mul.627, f32[2048,256]{1,0:T(8,128)S(1)} %bitcast.99, s32[256]{0:T(256)S(1)} %get-tuple-element.48), kind=kOutput, calls=%fused_computation.288 | convolution fusion | flops 25191422 | bytes 2130952 | tf_op jit(solution)/shard_map/dot_general | solution.py:28
  87.7 1.3 compare_select_fusion.18
  90.4 5.9 %all-to-all-done.2 = f32[128,16,128]{2,1,0:T(8,128)S(1)} async-done(((f32[128,16,128]{2,1,0:T(8,128)}), f32[128,16,128]{2,1,0:T(8,128)S(1)}, u32[]{:S(2)}, u32[]{:S(2)}) %all-to-all-start.2) | async-done | bytes 1048608 | tf_op jit(solution)/shard_map/all_to_all | solution.py:92
  96.3 5.6 %all-to-all-start.1 = ((f32[128,17,128]{2,1,0:T(8,128)}), f32[128,17,128]{2,1,0:T(8,128)}, u32[]{:S(2)}, u32[]{:S(2)}) async-start(f32[128,17,128]{2,1,0:T(8,128)} %pad_maximum_fusion), calls=%async_computation.1 | async-start | bytes 3145728 | tf_op jit(solution)/shard_map/all_to_all | solution.py:89
  106.2 1.3 select_add_fusion.9
  108.0 6.0 %fusion.17 = f32[4,4,64,256]{3,2,0,1:T(8,128)S(1)} fusion(f32[32,4,4,8,64]{4,3,2,1,0:T(8,128)S(1)} %reshape.647, f32[4,256]{1,0:T(4,128)S(1)} %copy.67, f32[256]{0:T(256)S(1)} %copy-done.4, f32[256]{0:T(256)S(1)} %copy-done.6, f32[256]{0:T(256)S(1)} %copy-done.8, f32[]{:T(128)} %bitcast.31, s32[256]{0:T(256)S(1)} %get-tuple-element.48, ...), kind=kOutput, calls=%fused_computation.25 | convolution fusion | flops 806748160 | bytes 2112528 | tf_op jit(solution)/shard_map/dot_general | solution.py:28
  114.1 5.4 %fusion.16 = f32[4,256,256]{2,1,0:T(8,128)} fusion(f32[4,4,64,256]{3,2,0,1:T(8,128)S(1)} %fusion.17, f32[256,256]{1,0:T(8,128)S(1)} %copy.69, f32[256]{0:T(256)S(1)} %get-tuple-element.52, f32[256]{0:T(256)S(1)} %get-tuple-element.53, f32[256]{0:T(256)S(1)} %copy-done.20, f32[]{:T(128)} %bitcast.41, s32[256]{0:T(256)S(1)} %get-tuple-element.48, ...), kind=kOutput, calls=%fused_computation.24 | convolution fusion | flops 806748160 | bytes 2370576 | tf_op jit(solution)/shard_map/dot_general | solution.py:28
  119.5 6.5 %all-to-all-done.1 = f32[128,17,128]{2,1,0:T(8,128)} async-done(((f32[128,17,128]{2,1,0:T(8,128)}), f32[128,17,128]{2,1,0:T(8,128)}, u32[]{:S(2)}, u32[]{:S(2)}) %all-to-all-start.1) | async-done | bytes 1114144 | tf_op jit(solution)/shard_map/all_to_all | solution.py:89
  126.0 2.0 %slice_reduce_fusion = (f32[]{:T(128)}, f32[]{:T(128)}) fusion(f32[128,17,128]{2,1,0:T(8,128)} %all-to-all-done.1), kind=kLoop, calls=%fused_computation.108 | loop fusion | flops 254 | bytes 1032 | tf_op jit(solution)/shard_map/reduce_sum | solution.py:94
  131.8 6.1 %fusion.20 = f32[4,4,64,256]{3,2,0,1:T(8,128)S(1)} fusion(f32[32,4,4,8,64]{4,3,2,1,0:T(8,128)S(1)} %reshape.646, f32[4,256]{1,0:T(4,128)S(1)} %copy.67, f32[256]{0:T(256)S(1)} %copy-done.4, f32[256]{0:T(256)S(1)} %copy-done.6, f32[256]{0:T(256)S(1)} %copy-done.8, f32[]{:T(128)} %bitcast.31, s32[256]{0:T(256)S(1)} %get-tuple-element.48, ...), kind=kOutput, calls=%fused_computation.26 | convolution fusion | flops 806748160 | bytes 2112528 | tf_op jit(solution)/shard_map/dot_general | solution.py:28
  137.9 4.4 %fusion.15 = f32[4,256,256]{2,1,0:T(8,128)S(1)} fusion(f32[4,4,64,256]{3,2,0,1:T(8,128)S(1)} %fusion.20, f32[256,256]{1,0:T(8,128)S(1)} %copy.69, f32[256]{0:T(256)S(1)} %get-tuple-element.52, f32[256]{0:T(256)S(1)} %get-tuple-element.53, f32[256]{0:T(256)S(1)} %copy-done.20, f32[]{:T(128)} %bitcast.41, s32[256]{0:T(256)S(1)} %get-tuple-element.48, ...), kind=kOutput, calls=%fused_computation.23 | convolution fusion | flops 806748160 | bytes 2370576 | tf_op jit(solution)/shard_map/dot_general | solution.py:28
  142.6 2.4 %copy.75 = f32[256,2,8,128]{3,1,2,0:T(2,128)} copy(f32[256,2,8,128]{3,2,1,0:T(8,128)S(1)} %bitcast.102) | data formatting | bytes 4194304
  (101 shorter events, 25.6 us)
Async XLA Ops:
  3.7 11.5 %copy-start.2 = (f32[2,16]{1,0:T(2,128)S(1)}, f32[2,16]{1,0:T(2,128)}, u32[]{:S(2)}) copy-start(f32[2,16]{1,0:T(2,128)} %param.3) | copy-start | bytes 388
  3.7 41.1 %all-to-all-start = ((f32[128,32,128]{2,1,0:T(8,128)}), f32[128,32,128]{2,1,0:T(8,128)S(1)}, u32[]{:S(2)}, u32[]{:S(2)}) async-start(f32[128,32,128]{2,1,0:T(8,128)} %copy.55), calls=%async_computation | async-start | bytes 4194304 | tf_op jit(solution)/shard_map/all_to_all | solution.py:40
  16.7 8.9 %copy-start.12 = (s32[4,64]{1,0:T(4,128)}, s32[4,64]{1,0:T(4,128)S(1)}, u32[]{:S(2)}) copy-start(s32[4,64]{1,0:T(4,128)S(1)} %get-tuple-element.42) | copy-start | bytes 3076
  16.7 8.9 %copy-start.14 = (s32[4,64]{1,0:T(4,128)}, s32[4,64]{1,0:T(4,128)S(1)}, u32[]{:S(2)}) copy-start(s32[4,64]{1,0:T(4,128)S(1)} %get-tuple-element.43) | copy-start | bytes 3076
  16.7 8.9 %copy-start.16 = (s32[4,64]{1,0:T(4,128)}, s32[4,64]{1,0:T(4,128)S(1)}, u32[]{:S(2)}) copy-start(s32[4,64]{1,0:T(4,128)S(1)} %get-tuple-element.44) | copy-start | bytes 3076
  16.7 8.9 %copy-start.18 = (s32[4,64]{1,0:T(4,128)}, s32[4,64]{1,0:T(4,128)S(1)}, u32[]{:S(2)}) copy-start(s32[4,64]{1,0:T(4,128)S(1)} %get-tuple-element.45) | copy-start | bytes 3076
  17.4 8.2 %copy-start.11 = (s32[1024]{0:T(1024)}, s32[1024]{0:T(1024)S(1)}, u32[]{:S(2)}) copy-start(s32[1024]{0:T(1024)S(1)} %pad_clamp_fusion.2) | copy-start | bytes 12292
  17.4 9.4 %copy-start.9 = (s32[1024]{0:T(1024)}, s32[1024]{0:T(1024)S(1)}, u32[]{:S(2)}) copy-start(s32[1024]{0:T(1024)S(1)} %pad_clamp_fusion.1) | copy-start | bytes 12292
  33.9 47.1 %copy-start.3 = (f32[256]{0:T(256)}, f32[256]{0:T(256)S(1)}, u32[]{:S(2)}) copy-start(f32[256]{0:T(256)S(1)} %get-tuple-element.55) | copy-start | bytes 3076
  72.3 24.0 %all-to-all-start.2 = ((f32[128,16,128]{2,1,0:T(8,128)}), f32[128,16,128]{2,1,0:T(8,128)S(1)}, u32[]{:S(2)}, u32[]{:S(2)}) async-start(f32[128,16,128]{2,1,0:T(8,128)} %get-tuple-element.7), calls=%async_computation.2 | async-start | bytes 2097152 | tf_op jit(solution)/shard_map/all_to_all | solution.py:92
  78.4 9.3 %copy-start.5 = (f32[256]{0:T(256)}, f32[256]{0:T(256)S(1)}, u32[]{:S(2)}) copy-start(f32[256]{0:T(256)S(1)} %get-tuple-element.56) | copy-start | bytes 3076
  78.4 9.3 %copy-start.7 = (f32[256]{0:T(256)}, f32[256]{0:T(256)S(1)}, u32[]{:S(2)}) copy-start(f32[256]{0:T(256)S(1)} %get-tuple-element.57) | copy-start | bytes 3076
  86.0 3.2 %copy-start = (f32[128,16,128]{2,1,0:T(8,128)S(1)}, f32[128,16,128]{2,1,0:T(8,128)}, u32[]{:S(2)}) copy-start(f32[128,16,128]{2,1,0:T(8,128)} %get-tuple-element.6) | copy-start | bytes 3145732
  90.4 12.2 %copy-start.10 = (s32[1024]{0:T(1024)S(1)}, s32[1024]{0:T(1024)}, u32[]{:S(2)}) copy-start(s32[1024]{0:T(1024)} %copy-done.9) | copy-start | bytes 12292
  96.3 29.7 %all-to-all-start.1 = ((f32[128,17,128]{2,1,0:T(8,128)}), f32[128,17,128]{2,1,0:T(8,128)}, u32[]{:S(2)}, u32[]{:S(2)}) async-start(f32[128,17,128]{2,1,0:T(8,128)} %pad_maximum_fusion), calls=%async_computation.1 | async-start | bytes 3145728 | tf_op jit(solution)/shard_map/all_to_all | solution.py:89
  106.0 2.0 %copy-start.4 = (f32[256]{0:T(256)S(1)}, f32[256]{0:T(256)}, u32[]{:S(2)}) copy-start(f32[256]{0:T(256)} %copy-done.3) | copy-start | bytes 3076
  106.0 2.0 %copy-start.6 = (f32[256]{0:T(256)S(1)}, f32[256]{0:T(256)}, u32[]{:S(2)}) copy-start(f32[256]{0:T(256)} %copy-done.5) | copy-start | bytes 3076
  106.0 2.0 %copy-start.8 = (f32[256]{0:T(256)S(1)}, f32[256]{0:T(256)}, u32[]{:S(2)}) copy-start(f32[256]{0:T(256)} %copy-done.7) | copy-start | bytes 3076
  107.9 6.1 %copy-start.13 = (s32[4,64]{1,0:T(4,128)S(1)}, s32[4,64]{1,0:T(4,128)}, u32[]{:S(2)}) copy-start(s32[4,64]{1,0:T(4,128)} %copy-done.12) | copy-start | bytes 3076
  107.9 6.1 %copy-start.15 = (s32[4,64]{1,0:T(4,128)S(1)}, s32[4,64]{1,0:T(4,128)}, u32[]{:S(2)}) copy-start(s32[4,64]{1,0:T(4,128)} %copy-done.14) | copy-start | bytes 3076
  108.0 6.1 %copy-start.17 = (s32[4,64]{1,0:T(4,128)S(1)}, s32[4,64]{1,0:T(4,128)}, u32[]{:S(2)}) copy-start(s32[4,64]{1,0:T(4,128)} %copy-done.16) | copy-start | bytes 3076
  108.0 6.1 %copy-start.19 = (s32[4,64]{1,0:T(4,128)S(1)}, s32[4,64]{1,0:T(4,128)}, u32[]{:S(2)}) copy-start(s32[4,64]{1,0:T(4,128)} %copy-done.18) | copy-start | bytes 3076
  108.0 6.1 %copy-start.20 = (f32[256]{0:T(256)S(1)}, f32[256]{0:T(256)}, u32[]{:S(2)}) copy-start(f32[256]{0:T(256)} %get-tuple-element.54) | copy-start | bytes 3076
  131.8 10.6 %copy-start.1 = (f32[4,256,256]{2,1,0:T(8,128)S(1)}, f32[4,256,256]{2,1,0:T(8,128)}, u32[]{:S(2)}) copy-start(f32[4,256,256]{2,1,0:T(8,128)} %fusion.16) | copy-start | bytes 3145732

commit v3 on v1

--- a/solution.py
+++ b/solution.py
@@ -24,14 +24,17 @@
     return (kernel, first_bond)
 
 
-def dot(lhs, rhs, lhs_dims, rhs_dims):
+def dot(lhs, rhs, lhs_dims, rhs_dims, precision=lax.Precision.HIGHEST):
     return lax.dot_general(
         lhs,
         rhs,
         ((lhs_dims, rhs_dims), ((), ())),
-        precision=lax.Precision.HIGHEST,
+        precision=precision,
         preferred_element_type=jnp.float32,
     )
+
+
+BLOCK_PRECISION = lax.Precision.HIGH
 
 
 def exchange(rows):
@@ -63,8 +66,8 @@
 
     received = exchange(state.reshape(-1, LANES).T)
     kernel1 = kernel1 * bond1[me % 4, column // quarter][None, :]
-    current = dot(received.reshape(spread, -1), kernel1, (0,), (0,))
-    current = dot(current.reshape(spread, -1, spread), kernel2, (0,), (0,))
+    current = dot(received.reshape(spread, -1), kernel1, (0,), (0,), BLOCK_PRECISION)
+    current = dot(current.reshape(spread, -1, spread), kernel2, (0,), (0,), BLOCK_PRECISION)
     pattern2 = bond2[column % 4][:, column // quarter]
     current = current * pattern2[None, :, :]
 
@@ -91,10 +94,10 @@
     received = received[:, :-1, :]
     current = received.reshape(devices // 4, 4, 8, per, quarter)
     kernel3 = kernel3.reshape(per, devices // 4, spread).transpose(1, 0, 2)
-    current = dot(current, kernel3, (0, 3), (0, 1))
+    current = dot(current, kernel3, (0, 3), (0, 1), BLOCK_PRECISION)
     pattern3 = bond3[jnp.arange(8) % 4][:, column // quarter]
     current = current * pattern3[None, :, None, :]
-    current = dot(current, kernel4.reshape(4, quarter, spread), (0, 2), (0, 1))
+    current = dot(current, kernel4.reshape(4, quarter, spread), (0, 2), (0, 1), BLOCK_PRECISION)
     pattern4 = bond4[column % 4][:, column // quarter]
 
     middle_mean = middle_total / whole_count

time: 146 us -> 139 us (0.952)
  matrix products: 35.4 us -> 27.9 us
    dot_general x7, matrix products: 35.4 us -> 27.9 us  [dot(): lax.dot_general(lhs, rhs, ((lhs_dims, rhs_dims), ((), ())), precision=pre...]
  transfers between devices with their start and end apart: 2 -> 2, of which waited for: 2 -> 2; matrix products, arithmetic and copies ran while one was open for 21% -> 23% of each run, Pallas kernels for 0% -> 0%
where the time goes in v3:
time: 139 us; the launch traced here: 138 us
  local copies, waits for them, and re-layouts  34.2 us (25%)
  waiting for transfers between devices  32.9 us (24%)
  matrix products  27.9 us (20%)
  other arithmetic  20.9 us (15%)
  starting transfers between devices  18 us (13%)
  between operations  4.24 us (3%)
    all_to_all x1, waiting for transfers between devices, shards(): lax.all_to_all(jnp.concatenate([sending, extra], axis=1), AXES, 0, 0, til...  29.6 us
    dot_general x7, matrix products, dot(): lax.dot_general(lhs, rhs, ((lhs_dims, rhs_dims), ((), ())), precision=pre...  27.9 us
    all_to_all x1, starting transfers between devices, exchange(): return lax.all_to_all(shaped, AXES, 0, 0, tiled=True).reshape(devices, -1)  11.5 us
    add x9, other arithmetic, block_kernel(): kernel = kernel * (1.0 + horizontal[level] * chained)[None, :]  9.22 us
    reshape x3, local copies, waits for them, and re-layouts, shards(): sending = current.reshape(per * quarter, -1).T.reshape(devices, -1, LANES)  7.17 us
    all_to_all x1, starting transfers between devices, shards(): lax.all_to_all(jnp.concatenate([sending, extra], axis=1), AXES, 0, 0, til...  6.48 us
    reshape x1, local copies, waits for them, and re-layouts, shards(): current = received.reshape(devices // 4, 4, 8, per, quarter)  4.33 us
    all_to_all x1, waiting for transfers between devices, exchange(): return lax.all_to_all(shaped, AXES, 0, 0, tiled=True).reshape(devices, -1)  3.31 us
  transfers between devices with their start and end apart: 2, of which 2 were waited for; matrix products, arithmetic and copies ran while one was open for 23% of the time, Pallas kernels for 0%

profile of v3, /device:TPU:1, one launch (start us, length us, event | category | flops | bytes accessed | tf_op | source)
XLA Modules:
  0.0 138.0 jit_solution(13910794433256386184)
XLA Ops:
  0.6 3.0 %copy.54 = f32[128,32,128]{2,1,0:T(8,128)} copy(f32[128,32,128]{0,2,1:T(8,128)} %bitcast.90) | data formatting | bytes 4194304 | tf_op jit(solution)/shard_map/reshape | solution.py:42
  3.7 11.5 %all-to-all-start = ((f32[128,32,128]{2,1,0:T(8,128)}), f32[128,32,128]{2,1,0:T(8,128)S(1)}, u32[]{:S(2)}, u32[]{:S(2)}) async-start(f32[128,32,128]{2,1,0:T(8,128)} %copy.54), calls=%async_computation | async-start | bytes 4194304 | tf_op jit(solution)/shard_map/all_to_all | solution.py:43
  18.1 1.2 select_add_fusion.3
  19.3 2.7 %multiply_reduce_fusion = f32[256,4]{0,1:T(4,128)S(1)} fusion(f32[4,64]{1,0:T(4,128)S(1)} %get-tuple-element.44, f32[4,64]{1,0:T(4,128)S(1)} %get-tuple-element.45, f32[4,64]{1,0:T(4,128)S(1)} %select_add_fusion.5, f32[]{:T(128)} %bitcast.41, s32[4,64]{1,0:T(4,128)S(1)} %get-tuple-element.40, s32[256]{0:T(256)S(1)} %get-tuple-element.46, f32[]{:T(128)} %bitcast.40, ...), kind=kLoop, calls=%fused_computation.83 | loop fusion | flops 1244160 | bytes 15376 | tf_op jit(solution)/shard_map/reduce_sum | solution.py:74
  22.8 1.0 gather_fusion.4
  25.5 1.1 select_add_fusion.11
  26.7 1.4 select_add_fusion.13
  28.9 1.0 gather_fusion.2
  32.5 1.1 fusion.42
  35.3 2.4 %gather_fusion = f32[256]{0:T(256)S(1)} fusion(f32[4,4]{1,0:T(4,128)S(1)} %select_add_fusion.8, s32[256]{0:T(256)S(1)} %bitcast.87), kind=kCustom, calls=%fused_computation | custom fusion | bytes 4096 | tf_op jit(solution)/shard_map/gather | solution.py:68
  39.0 1.2 select_add_fusion.18
  40.2 1.2 select_add_fusion.15
  41.4 3.3 %all-to-all-done = f32[128,32,128]{2,1,0:T(8,128)S(1)} async-done(((f32[128,32,128]{2,1,0:T(8,128)}), f32[128,32,128]{2,1,0:T(8,128)S(1)}, u32[]{:S(2)}, u32[]{:S(2)}) %all-to-all-start) | async-done | bytes 2097184 | tf_op jit(solution)/shard_map/all_to_all | solution.py:43
  44.7 1.5 %reshape_reshape.3 = f32[256,2048]{1,0:T(8,128)} reshape(f32[128,32,128]{2,1,0:T(8,128)S(1)} %all-to-all-done) | data formatting | bytes 4194304 | tf_op jit(solution)/shard_map/reshape;reshape | solution.py:69
  46.2 5.3 %convolution_bitcast_fusion = f32[2048,256]{0,1:T(8,128)S(1)} fusion(f32[256,2048]{1,0:T(8,128)} %reshape_reshape.3, f32[256]{0:T(256)S(1)} %gather_fusion, f32[256]{0:T(256)S(1)} %get-tuple-element.58, f32[256]{0:T(256)S(1)} %get-tuple-element.59, f32[256]{0:T(256)S(1)} %select_add_fusion.20, f32[]{:T(128)} %bitcast.3, s32[256]{0:T(256)S(1)} %get-tuple-element.46, ...), kind=kOutput, calls=%fused_computation.11 | convolution fusion | flops 806551552 | bytes 4202512 | tf_op jit(solution)/shard_map/dot_general | solution.py:28
  51.5 1.8 %copy.55 = f32[2048,256]{1,0:T(8,128)} copy(f32[2048,256]{0,1:T(8,128)S(1)} %convolution_bitcast_fusion) | data formatting | bytes 4194304 | tf_op jit(solution)/shard_map/dot_general | solution.py:28
  53.3 6.2 %fusion.6 = f32[8,256,256]{2,1,0:T(8,128)S(1)} fusion(f32[256,8,256]{2,1,0:T(8,128)} %bitcast.88, f32[256,256]{1,0:T(8,128)S(1)} %copy.58, f32[256]{0:T(256)S(1)} %get-tuple-element.56, f32[256]{0:T(256)S(1)} %get-tuple-element.57, f32[256]{0:T(256)S(1)} %select_add_fusion.17, f32[]{:T(128)} %bitcast.17, f32[]{:T(128)} %bitcast.16, f32[]{:T(128)} %bitcast.15, ...), kind=kOutput, calls=%fused_computation.19 | convolution fusion | flops 807010304 | bytes 4463632 | tf_op jit(solution)/shard_map/dot_general | solution.py:28
  59.5 1.6 %reshape.667 = f32[512,1024]{1,0:T(8,128)} reshape(f32[8,256,256]{2,1,0:T(8,128)S(1)} %fusion.6) | data formatting | bytes 4194304 | tf_op jit(solution)/shard_map/reshape | solution.py:87
  61.2 2.9 %copy.59 = f32[512,1024]{0,1:T(8,128)} copy(f32[512,1024]{1,0:T(8,128)} %reshape.667) | data formatting | bytes 4194304 | tf_op jit(solution)/shard_map/reshape | solution.py:87
  64.1 2.6 %reshape.668 = f32[128,32,128]{2,1,0:T(8,128)} reshape(f32[1024,512]{1,0:T(8,128)} %bitcast.89) | data formatting | bytes 4194304 | tf_op jit(solution)/shard_map/reshape | solution.py:87
  66.7 1.8 %fusion.218 = (f32[]{:T(128)}, f32[]{:T(128)}) fusion(f32[2048,4]{0,1:T(4,128)S(1)} %mul.605, f32[2048,256]{1,0:T(8,128)S(1)} %bitcast.86, s32[256]{0:T(256)S(1)} %get-tuple-element.46), kind=kOutput, calls=%fused_computation.347 | convolution fusion | flops 25191422 | bytes 2130952 | tf_op jit(solution)/shard_map/dot_general | solution.py:28
  68.5 1.3 compare_select_fusion.19
  69.8 1.7 %pad_maximum_fusion = f32[128,33,128]{2,1,0:T(8,128)} fusion(f32[128,1,128]{2,1,0:T(1,128)S(1)} %broadcast_in_dim.14, f32[128,32,128]{2,1,0:T(8,128)S(1)} %copy-done), kind=kLoop, calls=%fused_computation.12 | loop fusion | flops 540672 | bytes 4325376 | tf_op jit(solution)/shard_map/concatenate | solution.py:91
  71.5 6.5 %all-to-all-start.1 = ((f32[128,33,128]{2,1,0:T(8,128)}), f32[128,33,128]{2,1,0:T(8,128)S(1)}, u32[]{:S(2)}, u32[]{:S(2)}) async-start(f32[128,33,128]{2,1,0:T(8,128)} %pad_maximum_fusion), calls=%async_computation.1 | async-start | bytes 5242880 | tf_op jit(solution)/shard_map/all_to_all | solution.py:91
  80.9 1.0 gather_fusion.8
  82.1 1.2 select_add_fusion.9
  83.3 29.6 %all-to-all-done.1 = f32[128,33,128]{2,1,0:T(8,128)S(1)} async-done(((f32[128,33,128]{2,1,0:T(8,128)}), f32[128,33,128]{2,1,0:T(8,128)S(1)}, u32[]{:S(2)}, u32[]{:S(2)}) %all-to-all-start.1) | async-done | bytes 2162720 | tf_op jit(solution)/shard_map/all_to_all | solution.py:91
  115.8 1.6 %slice.230 = f32[128,32,128]{2,1,0:T(8,128)} slice(f32[128,33,128]{2,1,0:T(8,128)S(1)} %all-to-all-done.1), slice={[0:128], [0:32], [0:128]} | slice | bytes 4194304 | tf_op jit(solution)/shard_map/slice | solution.py:94
  117.4 4.3 %reshape.673 = f32[32,4,8,8,64]{4,3,2,1,0:T(8,128)} reshape(f32[128,32,128]{2,1,0:T(8,128)} %slice.230) | data formatting | bytes 4194304 | tf_op jit(solution)/shard_map/reshape | solution.py:95
  121.7 8.3 %fusion = f32[4,8,64,256,1]{3,2,4,0,1:T(8,128)S(1)} fusion(f32[32,4,8,8,64]{4,3,2,1,0:T(8,128)} %reshape.673, f32[256]{0:T(256)S(1)} %get-tuple-element.53, f32[256]{0:T(256)S(1)} %get-tuple-element.54, f32[256]{0:T(256)S(1)} %get-tuple-element.55, f32[]{:T(128)} %bitcast.31, s32[256]{0:T(256)S(1)} %get-tuple-element.46, s32[32,8]{1,0:T(8,128)S(1)} %get-tuple-element.60, ...), kind=kOutput, calls=%fused_computation.9 | convolution fusion | flops 806486016 | bytes 4205584 | tf_op jit(solution)/shard_map/dot_general | solution.py:28
  130.0 4.5 %fusion.2 = f32[8,256,256]{2,1,0:T(8,128)S(1)} fusion(f32[4,8,64,256,1]{3,2,4,0,1:T(8,128)S(1)} %fusion, f32[]{:T(128)S(6)} %mul.652, f32[256,256]{1,0:T(8,128)S(1)} %copy.68, f32[8,256]{1,0:T(8,128)S(1)} %copy.66, f32[256]{0:T(256)S(1)} %get-tuple-element.50, f32[256]{0:T(256)S(1)} %get-tuple-element.51, f32[256]{0:T(256)S(1)} %get-tuple-element.52, ...), kind=kOutput, calls=%fused_computation.14 | convolution fusion | flops 808058880 | bytes 4475924 | tf_op jit(solution)/shard_map/dot_general | solution.py:28
  134.5 2.4 %copy.71 = f32[256,2,8,128]{3,1,2,0:T(2,128)} copy(f32[256,2,8,128]{3,2,1,0:T(8,128)S(1)} %bitcast.91) | data formatting | bytes 4194304
  (56 shorter events, 15.5 us)
Async XLA Ops:
  3.7 11.5 %copy-start.1 = (f32[2,16]{1,0:T(2,128)S(1)}, f32[2,16]{1,0:T(2,128)}, u32[]{:S(2)}) copy-start(f32[2,16]{1,0:T(2,128)} %param.3) | copy-start | bytes 388
  3.7 41.1 %all-to-all-start = ((f32[128,32,128]{2,1,0:T(8,128)}), f32[128,32,128]{2,1,0:T(8,128)S(1)}, u32[]{:S(2)}, u32[]{:S(2)}) async-start(f32[128,32,128]{2,1,0:T(8,128)} %copy.54), calls=%async_computation | async-start | bytes 4194304 | tf_op jit(solution)/shard_map/all_to_all | solution.py:43
  66.7 3.1 %copy-start = (f32[128,32,128]{2,1,0:T(8,128)S(1)}, f32[128,32,128]{2,1,0:T(8,128)}, u32[]{:S(2)}) copy-start(f32[128,32,128]{2,1,0:T(8,128)} %reshape.668) | copy-start | bytes 6291460
  71.5 41.4 %all-to-all-start.1 = ((f32[128,33,128]{2,1,0:T(8,128)}), f32[128,33,128]{2,1,0:T(8,128)S(1)}, u32[]{:S(2)}, u32[]{:S(2)}) async-start(f32[128,33,128]{2,1,0:T(8,128)} %pad_maximum_fusion), calls=%async_computation.1 | async-start | bytes 5242880 | tf_op jit(solution)/shard_map/all_to_all | solution.py:91

commit v4 on v3

--- a/solution.py
+++ b/solution.py
@@ -64,12 +64,14 @@
     (kernel1, bond1), (kernel2, bond2), (kernel3, bond3), (kernel4, bond4) = kernels
     column = jnp.arange(spread, dtype=jnp.int32)
 
-    received = exchange(state.reshape(-1, LANES).T)
+    sending = jnp.transpose(state.reshape(2, spread, -1, LANES), (3, 0, 2, 1))
+    received = exchange(sending.reshape(devices, -1))
     kernel1 = kernel1 * bond1[me % 4, column // quarter][None, :]
-    current = dot(received.reshape(spread, -1), kernel1, (0,), (0,), BLOCK_PRECISION)
-    current = dot(current.reshape(spread, -1, spread), kernel2, (0,), (0,), BLOCK_PRECISION)
+    current = dot(kernel1, received.reshape(spread, -1), (0,), (0,), BLOCK_PRECISION)
+    current = dot(current.reshape(-1, spread), kernel2, (1,), (0,), BLOCK_PRECISION)
     pattern2 = bond2[column % 4][:, column // quarter]
-    current = current * pattern2[None, :, :]
+    current = current.reshape(spread, -1, spread) * pattern2[:, None, :]
+    current = jnp.transpose(current, (1, 0, 2))
 
     tail = kernel4.reshape(spread, 4, quarter).sum(axis=2)
     tail = dot(tail, bond4, (1,), (1,))

time: 139 us -> 137 us (0.986)
  matrix products: 27.9 us -> 24.5 us
    dot_general x7, matrix products: 27.9 us -> 24.5 us  [dot(): lax.dot_general(lhs, rhs, ((lhs_dims, rhs_dims), ((), ())), precision=pre...]
    reshape x1 -> x0, local copies, waits for them, and re-layouts: 3.04 us -> none  [exchange(): shaped = rows.reshape(devices, -1, LANES)]
    transpose x0 -> x1, local copies, waits for them, and re-layouts: none -> 2 us  [shards(): sending = jnp.transpose(state.reshape(2, spread, -1, LANES), (3, 0, 2, 1))]
    another operation x1 -> x2, local copies, waits for them, and re-layouts: 0.08 us -> 2.04 us  [the longest x1 1.97 us: exchange(): shaped = rows.reshape(devices, -1, LANES)]
    add x9 -> x8, other arithmetic: 9.22 us -> 9.62 us  [block_kernel(): kernel = kernel * (1.0 + horizontal[level] * chained)[None, :]]
where the time goes in v4:
time: 137 us; the launch traced here: 136 us
  local copies, waits for them, and re-layouts  35.2 us (26%)
  waiting for transfers between devices  32.6 us (24%)
  matrix products  24.5 us (18%)
  other arithmetic  21.1 us (15%)
  starting transfers between devices  18.2 us (13%)
  between operations  4.25 us (3%)
    all_to_all x1, waiting for transfers between devices, shards(): lax.all_to_all(jnp.concatenate([sending, extra], axis=1), AXES, 0, 0, til...  29.5 us
    dot_general x7, matrix products, dot(): lax.dot_general(lhs, rhs, ((lhs_dims, rhs_dims), ((), ())), precision=pre...  24.5 us
    all_to_all x1, starting transfers between devices, exchange(): return lax.all_to_all(shaped, AXES, 0, 0, tiled=True).reshape(devices, -1)  11.5 us
    add x8, other arithmetic, block_kernel(): kernel = kernel * (1.0 + horizontal[level] * chained)[None, :]  9.62 us
    reshape x3, local copies, waits for them, and re-layouts, shards(): sending = current.reshape(per * quarter, -1).T.reshape(devices, -1, LANES)  7.17 us
    all_to_all x1, starting transfers between devices, shards(): lax.all_to_all(jnp.concatenate([sending, extra], axis=1), AXES, 0, 0, til...  6.72 us
    reshape x1, local copies, waits for them, and re-layouts, shards(): current = received.reshape(devices // 4, 4, 8, per, quarter)  4.35 us
    all_to_all x1, waiting for transfers between devices, exchange(): return lax.all_to_all(shaped, AXES, 0, 0, tiled=True).reshape(devices, -1)  3.07 us
  transfers between devices with their start and end apart: 2, of which 2 were waited for; matrix products, arithmetic and copies ran while one was open for 23% of the time, Pallas kernels for 0%

profile of v4, /device:TPU:1, one launch (start us, length us, event | category | flops | bytes accessed | tf_op | source)
XLA Modules:
  0.0 135.8 jit_solution(1467389605360035190)
XLA Ops:
  0.6 2.0 %copy.69 = f32[128,2,8,256]{0,3,2,1:T(8,128)S(1)} copy(f32[128,2,8,256]{0,2,3,1:T(8,128)} %bitcast.97) | data formatting | bytes 4194304 | tf_op jit(solution)/shard_map/transpose | solution.py:67
  2.6 2.0 %copy.70 = f32[128,32,128]{2,1,0:T(8,128)} copy(f32[128,32,128]{0,2,1:T(8,128)S(1)} %bitcast.96) | data formatting | bytes 4194304 | tf_op jit(solution)/shard_map/reshape;reshape | solution.py:42
  4.6 11.5 %all-to-all-start = ((f32[128,32,128]{2,1,0:T(8,128)}), f32[128,32,128]{2,1,0:T(8,128)S(1)}, u32[]{:S(2)}, u32[]{:S(2)}) async-start(f32[128,32,128]{2,1,0:T(8,128)} %copy.70), calls=%async_computation | async-start | bytes 4194304 | tf_op jit(solution)/shard_map/all_to_all | solution.py:43
  19.0 1.3 select_add_fusion.3
  20.2 2.8 %multiply_reduce_fusion = f32[256,4]{0,1:T(4,128)S(1)} fusion(f32[4,64]{1,0:T(4,128)S(1)} %get-tuple-element.44, f32[4,64]{1,0:T(4,128)S(1)} %get-tuple-element.45, f32[4,64]{1,0:T(4,128)S(1)} %select_add_fusion.5, f32[]{:T(128)} %bitcast.43, s32[4,64]{1,0:T(4,128)S(1)} %get-tuple-element.40, s32[256]{0:T(256)S(1)} %get-tuple-element.46, f32[]{:T(128)} %bitcast.42, ...), kind=kLoop, calls=%fused_computation.82 | loop fusion | flops 1244160 | bytes 15376 | tf_op jit(solution)/shard_map/reduce_sum | solution.py:76
  26.4 1.4 %select_add_fusion.11 = (f32[256]{0:T(256)S(1)}, f32[256]{0:T(256)S(1)}) fusion(f32[]{:T(128)} %bitcast.44, f32[]{:T(128)} %bitcast.36), kind=kLoop, calls=%fused_computation.319 | loop fusion | flops 16128 | bytes 2056 | tf_op jit(solution)/shard_map/add | solution.py:21
  27.9 1.4 %select_add_fusion.13 = (f32[256]{0:T(256)S(1)}, f32[256]{0:T(256)S(1)}) fusion(f32[]{:T(128)} %bitcast.35, f32[]{:T(128)} %bitcast.34), kind=kLoop, calls=%fused_computation.321 | loop fusion | flops 15104 | bytes 2056 | tf_op jit(solution)/shard_map/add | solution.py:21
  33.7 1.1 fusion.39
  36.5 2.4 %gather_fusion = f32[256]{0:T(256)S(1)} fusion(f32[4,4]{1,0:T(4,128)S(1)} %select_add_fusion.8, s32[256]{0:T(256)S(1)} %bitcast.92), kind=kCustom, calls=%fused_computation | custom fusion | bytes 4096 | tf_op jit(solution)/shard_map/gather | solution.py:69
  39.0 1.1 select_add_fusion.17
  40.1 1.3 select_add_fusion.19
  41.3 1.2 select_add_fusion.15
  42.6 3.1 %all-to-all-done = f32[128,32,128]{2,1,0:T(8,128)S(1)} async-done(((f32[128,32,128]{2,1,0:T(8,128)}), f32[128,32,128]{2,1,0:T(8,128)S(1)}, u32[]{:S(2)}, u32[]{:S(2)}) %all-to-all-start) | async-done | bytes 2097184 | tf_op jit(solution)/shard_map/all_to_all | solution.py:43
  45.7 1.5 %reshape_reshape.7 = f32[256,2048]{1,0:T(8,128)} reshape(f32[128,32,128]{2,1,0:T(8,128)S(1)} %all-to-all-done) | data formatting | bytes 4194304 | tf_op jit(solution)/shard_map/reshape;reshape | solution.py:70
  47.1 1.9 %copy.71 = f32[2048,256]{1,0:T(8,128)S(1)} copy(f32[2048,256]{0,1:T(8,128)} %bitcast.94) | data formatting | bytes 4194304 | tf_op jit(solution)/shard_map/dot_general | solution.py:28
  49.1 4.4 %fusion.14 = f32[256,8,256]{2,0,1:T(8,128)S(1)} fusion(f32[8,256,256]{2,1,0:T(8,128)S(1)} %bitcast.93, f32[256]{0:T(256)S(1)} %gather_fusion, f32[256]{0:T(256)S(1)} %get-tuple-element.59, f32[256]{0:T(256)S(1)} %get-tuple-element.60, f32[256]{0:T(256)S(1)} %get-tuple-element.61, f32[]{:T(128)} %bitcast.3, s32[256]{0:T(256)S(1)} %get-tuple-element.46, ...), kind=kOutput, calls=%fused_computation.35 | convolution fusion | flops 806551552 | bytes 4202512 | tf_op jit(solution)/shard_map/dot_general | solution.py:28
  53.5 3.6 %convolution_multiply_fusion = f32[256,8,256]{2,0,1:T(8,128)S(1)} fusion(f32[256,8,256]{2,0,1:T(8,128)S(1)} %fusion.14, f32[256,256]{1,0:T(8,128)S(1)} %copy.74, f32[256]{0:T(256)S(1)} %get-tuple-element.56, f32[256]{0:T(256)S(1)} %get-tuple-element.57, f32[256]{0:T(256)S(1)} %get-tuple-element.58, f32[]{:T(128)} %bitcast.18, f32[]{:T(128)} %bitcast.17, ...), kind=kOutput, calls=%fused_computation.16 | convolution fusion | flops 807010304 | bytes 4463632 | tf_op jit(solution)/shard_map/dot_general | solution.py:28
  57.1 1.6 %reshape.664 = f32[512,1024]{1,0:T(8,128)} reshape(f32[8,256,256]{2,1,0:T(8,128)S(1)} %bitcast.90) | data formatting | bytes 4194304 | tf_op jit(solution)/shard_map/reshape | solution.py:89
  58.7 2.9 %copy.75 = f32[512,1024]{0,1:T(8,128)} copy(f32[512,1024]{1,0:T(8,128)} %reshape.664) | data formatting | bytes 4194304 | tf_op jit(solution)/shard_map/reshape | solution.py:89
  61.7 2.6 %reshape.665 = f32[128,32,128]{2,1,0:T(8,128)} reshape(f32[1024,512]{1,0:T(8,128)} %bitcast.95) | data formatting | bytes 4194304 | tf_op jit(solution)/shard_map/reshape | solution.py:89
  64.3 1.7 %fusion.215 = (f32[]{:T(128)}, f32[]{:T(128)}) fusion(f32[2048,4]{0,1:T(4,128)S(1)} %mul.610, f32[2048,256]{1,0:T(8,128)S(1)} %bitcast.91, s32[256]{0:T(256)S(1)} %get-tuple-element.46), kind=kOutput, calls=%fused_computation.346 | convolution fusion | flops 25191422 | bytes 2130952 | tf_op jit(solution)/shard_map/dot_general | solution.py:28
  66.0 1.2 compare_select_fusion.19
  67.3 1.7 %pad_maximum_fusion = f32[128,33,128]{2,1,0:T(8,128)} fusion(f32[128,1,128]{2,1,0:T(1,128)S(1)} %broadcast_in_dim.14, f32[128,32,128]{2,1,0:T(8,128)S(1)} %copy-done), kind=kLoop, calls=%fused_computation.11 | loop fusion | flops 540672 | bytes 4325376 | tf_op jit(solution)/shard_map/concatenate | solution.py:93
  69.0 6.7 %all-to-all-start.1 = ((f32[128,33,128]{2,1,0:T(8,128)}), f32[128,33,128]{2,1,0:T(8,128)S(1)}, u32[]{:S(2)}, u32[]{:S(2)}) async-start(f32[128,33,128]{2,1,0:T(8,128)} %pad_maximum_fusion), calls=%async_computation.1 | async-start | bytes 5242880 | tf_op jit(solution)/shard_map/all_to_all | solution.py:93
  78.6 1.0 gather_fusion.8
  79.8 1.3 select_add_fusion.9
  81.1 29.5 %all-to-all-done.1 = f32[128,33,128]{2,1,0:T(8,128)S(1)} async-done(((f32[128,33,128]{2,1,0:T(8,128)}), f32[128,33,128]{2,1,0:T(8,128)S(1)}, u32[]{:S(2)}, u32[]{:S(2)}) %all-to-all-start.1) | async-done | bytes 2162720 | tf_op jit(solution)/shard_map/all_to_all | solution.py:93
  113.5 1.6 %slice.230 = f32[128,32,128]{2,1,0:T(8,128)} slice(f32[128,33,128]{2,1,0:T(8,128)S(1)} %all-to-all-done.1), slice={[0:128], [0:32], [0:128]} | slice | bytes 4194304 | tf_op jit(solution)/shard_map/slice | solution.py:96
  115.1 4.3 %reshape.670 = f32[32,4,8,8,64]{4,3,2,1,0:T(8,128)} reshape(f32[128,32,128]{2,1,0:T(8,128)} %slice.230) | data formatting | bytes 4194304 | tf_op jit(solution)/shard_map/reshape | solution.py:97
  119.4 8.3 %fusion = f32[4,8,64,256,1]{3,2,4,0,1:T(8,128)S(1)} fusion(f32[32,4,8,8,64]{4,3,2,1,0:T(8,128)} %reshape.670, f32[256]{0:T(256)S(1)} %get-tuple-element.53, f32[256]{0:T(256)S(1)} %get-tuple-element.54, f32[256]{0:T(256)S(1)} %get-tuple-element.55, f32[]{:T(128)} %bitcast.33, s32[256]{0:T(256)S(1)} %get-tuple-element.46, s32[32,8]{1,0:T(8,128)S(1)} %get-tuple-element.62, ...), kind=kOutput, calls=%fused_computation.9 | convolution fusion | flops 806486016 | bytes 4205584 | tf_op jit(solution)/shard_map/dot_general | solution.py:28
  127.7 4.6 %fusion.2 = f32[8,256,256]{2,1,0:T(8,128)S(1)} fusion(f32[4,8,64,256,1]{3,2,4,0,1:T(8,128)S(1)} %fusion, f32[]{:T(128)S(6)} %mul.657, f32[256,256]{1,0:T(8,128)S(1)} %copy.84, f32[8,256]{1,0:T(8,128)S(1)} %copy.82, f32[256]{0:T(256)S(1)} %get-tuple-element.50, f32[256]{0:T(256)S(1)} %get-tuple-element.51, f32[256]{0:T(256)S(1)} %get-tuple-element.52, ...), kind=kOutput, calls=%fused_computation.13 | convolution fusion | flops 808058880 | bytes 4475924 | tf_op jit(solution)/shard_map/dot_general | solution.py:28
  132.3 2.4 %copy.89 = f32[256,2,8,128]{3,1,2,0:T(2,128)} copy(f32[256,2,8,128]{3,2,1,0:T(8,128)S(1)} %bitcast.98) | data formatting | bytes 4194304
  (56 shorter events, 16.1 us)
Async XLA Ops:
  4.6 11.5 %copy-start.1 = (f32[2,16]{1,0:T(2,128)S(1)}, f32[2,16]{1,0:T(2,128)}, u32[]{:S(2)}) copy-start(f32[2,16]{1,0:T(2,128)} %param.3) | copy-start | bytes 388
  4.6 41.1 %all-to-all-start = ((f32[128,32,128]{2,1,0:T(8,128)}), f32[128,32,128]{2,1,0:T(8,128)S(1)}, u32[]{:S(2)}, u32[]{:S(2)}) async-start(f32[128,32,128]{2,1,0:T(8,128)} %copy.70), calls=%async_computation | async-start | bytes 4194304 | tf_op jit(solution)/shard_map/all_to_all | solution.py:43
  64.3 3.0 %copy-start = (f32[128,32,128]{2,1,0:T(8,128)S(1)}, f32[128,32,128]{2,1,0:T(8,128)}, u32[]{:S(2)}) copy-start(f32[128,32,128]{2,1,0:T(8,128)} %reshape.665) | copy-start | bytes 6291460
  69.0 41.6 %all-to-all-start.1 = ((f32[128,33,128]{2,1,0:T(8,128)}), f32[128,33,128]{2,1,0:T(8,128)S(1)}, u32[]{:S(2)}, u32[]{:S(2)}) async-start(f32[128,33,128]{2,1,0:T(8,128)} %pad_maximum_fusion), calls=%async_computation.1 | async-start | bytes 5242880 | tf_op jit(solution)/shard_map/all_to_all | solution.py:93

commit v5 on v4

--- a/solution.py
+++ b/solution.py
@@ -65,9 +65,9 @@
     column = jnp.arange(spread, dtype=jnp.int32)
 
     sending = jnp.transpose(state.reshape(2, spread, -1, LANES), (3, 0, 2, 1))
-    received = exchange(sending.reshape(devices, -1))
+    received = lax.all_to_all(sending, AXES, 0, 0, tiled=True)
     kernel1 = kernel1 * bond1[me % 4, column // quarter][None, :]
-    current = dot(kernel1, received.reshape(spread, -1), (0,), (0,), BLOCK_PRECISION)
+    current = dot(kernel1, received.reshape(spread, -1, spread), (0,), (0,), BLOCK_PRECISION)
     current = dot(current.reshape(-1, spread), kernel2, (1,), (0,), BLOCK_PRECISION)
     pattern2 = bond2[column % 4][:, column // quarter]
     current = current.reshape(spread, -1, spread) * pattern2[:, None, :]

time: 137 us -> 132 us (0.964)
  local copies, waits for them, and re-layouts: 35.2 us -> 31 us
    another operation x3 -> x1, local copies, waits for them, and re-layouts: 3.52 us -> 0.08 us  [the longest x1 1.97 us: exchange(): shaped = rows.reshape(devices, -1, LANES)]
    dot_general x1 -> x0, local copies, waits for them, and re-layouts: 1.92 us -> none  [dot(): lax.dot_general(lhs, rhs, ((lhs_dims, rhs_dims), ((), ())), precision=pre...]
  transfers between devices with their start and end apart: 2 -> 2, of which waited for: 2 -> 2; matrix products, arithmetic and copies ran while one was open for 23% -> 24% of each run, Pallas kernels for 0% -> 0%
where the time goes in v5:
time: 132 us; the launch traced here: 131 us
  waiting for transfers between devices  32.6 us (25%)
  local copies, waits for them, and re-layouts  31 us (23%)
  matrix products  24.2 us (18%)
  other arithmetic  21.1 us (16%)
  starting transfers between devices  18.2 us (14%)
  between operations  4.24 us (3%)
    all_to_all x1, waiting for transfers between devices, shards(): lax.all_to_all(jnp.concatenate([sending, extra], axis=1), AXES, 0, 0, til...  29.5 us
    dot_general x7, matrix products, dot(): lax.dot_general(lhs, rhs, ((lhs_dims, rhs_dims), ((), ())), precision=pre...  24.2 us
    all_to_all x1, starting transfers between devices, shards(): received = lax.all_to_all(sending, AXES, 0, 0, tiled=True)  11.5 us
    add x8, other arithmetic, block_kernel(): kernel = kernel * (1.0 + horizontal[level] * chained)[None, :]  9.62 us
    reshape x3, local copies, waits for them, and re-layouts, shards(): sending = current.reshape(per * quarter, -1).T.reshape(devices, -1, LANES)  7.17 us
    all_to_all x1, starting transfers between devices, shards(): lax.all_to_all(jnp.concatenate([sending, extra], axis=1), AXES, 0, 0, til...  6.71 us
    reshape x1, local copies, waits for them, and re-layouts, shards(): current = received.reshape(devices // 4, 4, 8, per, quarter)  4.35 us
    transpose x1, local copies, waits for them, and re-layouts, shards(): sending = jnp.transpose(state.reshape(2, spread, -1, LANES), (3, 0, 2, 1))  3.11 us
  transfers between devices with their start and end apart: 2, of which 2 were waited for; matrix products, arithmetic and copies ran while one was open for 24% of the time, Pallas kernels for 0%

profile of v5, /device:TPU:1, one launch (start us, length us, event | category | flops | bytes accessed | tf_op | source)
XLA Modules:
  0.0 131.3 jit_solution(15408869700611804896)
XLA Ops:
  0.6 3.1 %copy.82 = f32[128,2,8,256]{3,2,1,0:T(8,128)} copy(f32[128,2,8,256]{0,2,3,1:T(8,128)} %bitcast.92) | data formatting | bytes 4194304 | tf_op jit(solution)/shard_map/transpose | solution.py:67
  3.7 11.5 %all-to-all-start = ((f32[128,2,8,256]{3,2,1,0:T(8,128)}), f32[128,2,8,256]{3,2,1,0:T(8,128)S(1)}, u32[]{:S(2)}, u32[]{:S(2)}) async-start(f32[128,2,8,256]{3,2,1,0:T(8,128)} %copy.82), calls=%async_computation | async-start | bytes 4194304 | tf_op jit(solution)/shard_map/all_to_all | solution.py:68
  18.1 1.3 select_add_fusion.3
  19.4 2.8 %multiply_reduce_fusion = f32[256,4]{0,1:T(4,128)S(1)} fusion(f32[4,64]{1,0:T(4,128)S(1)} %get-tuple-element.44, f32[4,64]{1,0:T(4,128)S(1)} %get-tuple-element.45, f32[4,64]{1,0:T(4,128)S(1)} %select_add_fusion.5, f32[]{:T(128)} %bitcast.41, s32[4,64]{1,0:T(4,128)S(1)} %get-tuple-element.40, s32[256]{0:T(256)S(1)} %get-tuple-element.46, f32[]{:T(128)} %bitcast.40, ...), kind=kLoop, calls=%fused_computation.83 | loop fusion | flops 1244160 | bytes 15376 | tf_op jit(solution)/shard_map/reduce_sum | solution.py:76
  23.0 1.0 gather_fusion.4
  25.6 1.4 %select_add_fusion.11 = (f32[256]{0:T(256)S(1)}, f32[256]{0:T(256)S(1)}) fusion(f32[]{:T(128)} %bitcast.42, f32[]{:T(128)} %bitcast.34), kind=kLoop, calls=%fused_computation.320 | loop fusion | flops 16128 | bytes 2056 | tf_op jit(solution)/shard_map/add | solution.py:21
  27.0 1.4 %select_add_fusion.13 = (f32[256]{0:T(256)S(1)}, f32[256]{0:T(256)S(1)}) fusion(f32[]{:T(128)} %bitcast.33, f32[]{:T(128)} %bitcast.32), kind=kLoop, calls=%fused_computation.322 | loop fusion | flops 15104 | bytes 2056 | tf_op jit(solution)/shard_map/add | solution.py:21
  29.2 1.0 gather_fusion.2
  32.9 1.1 fusion.40
  35.7 2.4 %gather_fusion = f32[256]{0:T(256)S(1)} fusion(f32[4,4]{1,0:T(4,128)S(1)} %select_add_fusion.8, s32[256]{0:T(256)S(1)} %bitcast.89), kind=kCustom, calls=%fused_computation | custom fusion | bytes 4096 | tf_op jit(solution)/shard_map/gather | solution.py:69
  38.1 1.1 select_add_fusion.17
  39.2 1.3 select_add_fusion.19
  40.5 1.2 select_add_fusion.15
  41.7 3.1 %all-to-all-done = f32[128,2,8,256]{3,2,1,0:T(8,128)S(1)} async-done(((f32[128,2,8,256]{3,2,1,0:T(8,128)}), f32[128,2,8,256]{3,2,1,0:T(8,128)S(1)}, u32[]{:S(2)}, u32[]{:S(2)}) %all-to-all-start) | async-done | bytes 2097184 | tf_op jit(solution)/shard_map/all_to_all | solution.py:68
  44.8 4.2 %fusion.4 = f32[256,8,256]{2,0,1:T(8,128)S(1)} fusion(f32[256,8,256]{2,1,0:T(8,128)S(1)} %bitcast.90, f32[256]{0:T(256)S(1)} %gather_fusion, f32[256]{0:T(256)S(1)} %get-tuple-element.59, f32[256]{0:T(256)S(1)} %get-tuple-element.60, f32[256]{0:T(256)S(1)} %get-tuple-element.61, f32[]{:T(128)} %bitcast.3, s32[256]{0:T(256)S(1)} %get-tuple-element.46, ...), kind=kOutput, calls=%fused_computation.16 | convolution fusion | flops 806551552 | bytes 4202512 | tf_op jit(solution)/shard_map/dot_general | solution.py:28
  49.0 3.6 %convolution_multiply_fusion = f32[256,8,256]{2,0,1:T(8,128)S(1)} fusion(f32[256,8,256]{2,0,1:T(8,128)S(1)} %fusion.4, f32[256,256]{1,0:T(8,128)S(1)} %copy.86, f32[256]{0:T(256)S(1)} %get-tuple-element.56, f32[256]{0:T(256)S(1)} %get-tuple-element.57, f32[256]{0:T(256)S(1)} %get-tuple-element.58, f32[]{:T(128)} %bitcast.16, f32[]{:T(128)} %bitcast.15, ...), kind=kOutput, calls=%fused_computation.18 | convolution fusion | flops 807010304 | bytes 4463632 | tf_op jit(solution)/shard_map/dot_general | solution.py:28
  52.6 1.6 %reshape.667 = f32[512,1024]{1,0:T(8,128)} reshape(f32[8,256,256]{2,1,0:T(8,128)S(1)} %bitcast.87) | data formatting | bytes 4194304 | tf_op jit(solution)/shard_map/reshape | solution.py:89
  54.2 2.9 %copy.87 = f32[512,1024]{0,1:T(8,128)} copy(f32[512,1024]{1,0:T(8,128)} %reshape.667) | data formatting | bytes 4194304 | tf_op jit(solution)/shard_map/reshape | solution.py:89
  57.2 2.6 %reshape.668 = f32[128,32,128]{2,1,0:T(8,128)} reshape(f32[1024,512]{1,0:T(8,128)} %bitcast.91) | data formatting | bytes 4194304 | tf_op jit(solution)/shard_map/reshape | solution.py:89
  59.8 1.7 %fusion.216 = (f32[]{:T(128)}, f32[]{:T(128)}) fusion(f32[2048,4]{0,1:T(4,128)S(1)} %mul.610, f32[2048,256]{1,0:T(8,128)S(1)} %bitcast.88, s32[256]{0:T(256)S(1)} %get-tuple-element.46), kind=kOutput, calls=%fused_computation.347 | convolution fusion | flops 25191422 | bytes 2130952 | tf_op jit(solution)/shard_map/dot_general | solution.py:28
  61.5 1.2 compare_select_fusion.19
  62.8 1.7 %pad_maximum_fusion = f32[128,33,128]{2,1,0:T(8,128)} fusion(f32[128,1,128]{2,1,0:T(1,128)S(1)} %broadcast_in_dim.14, f32[128,32,128]{2,1,0:T(8,128)S(1)} %copy-done), kind=kLoop, calls=%fused_computation.11 | loop fusion | flops 540672 | bytes 4325376 | tf_op jit(solution)/shard_map/concatenate | solution.py:93
  64.5 6.7 %all-to-all-start.1 = ((f32[128,33,128]{2,1,0:T(8,128)}), f32[128,33,128]{2,1,0:T(8,128)S(1)}, u32[]{:S(2)}, u32[]{:S(2)}) async-start(f32[128,33,128]{2,1,0:T(8,128)} %pad_maximum_fusion), calls=%async_computation.1 | async-start | bytes 5242880 | tf_op jit(solution)/shard_map/all_to_all | solution.py:93
  74.1 1.0 gather_fusion.8
  75.2 1.3 select_add_fusion.9
  76.6 29.5 %all-to-all-done.1 = f32[128,33,128]{2,1,0:T(8,128)S(1)} async-done(((f32[128,33,128]{2,1,0:T(8,128)}), f32[128,33,128]{2,1,0:T(8,128)S(1)}, u32[]{:S(2)}, u32[]{:S(2)}) %all-to-all-start.1) | async-done | bytes 2162720 | tf_op jit(solution)/shard_map/all_to_all | solution.py:93
  106.1 0.8 slice_reduce_fusion
  108.9 1.6 %slice.230 = f32[128,32,128]{2,1,0:T(8,128)} slice(f32[128,33,128]{2,1,0:T(8,128)S(1)} %all-to-all-done.1), slice={[0:128], [0:32], [0:128]} | slice | bytes 4194304 | tf_op jit(solution)/shard_map/slice | solution.py:96
  110.6 4.3 %reshape.673 = f32[32,4,8,8,64]{4,3,2,1,0:T(8,128)} reshape(f32[128,32,128]{2,1,0:T(8,128)} %slice.230) | data formatting | bytes 4194304 | tf_op jit(solution)/shard_map/reshape | solution.py:97
  114.9 8.3 %fusion = f32[4,8,64,256,1]{3,2,4,0,1:T(8,128)S(1)} fusion(f32[32,4,8,8,64]{4,3,2,1,0:T(8,128)} %reshape.673, f32[256]{0:T(256)S(1)} %get-tuple-element.53, f32[256]{0:T(256)S(1)} %get-tuple-element.54, f32[256]{0:T(256)S(1)} %get-tuple-element.55, f32[]{:T(128)} %bitcast.31, s32[256]{0:T(256)S(1)} %get-tuple-element.46, s32[32,8]{1,0:T(8,128)S(1)} %get-tuple-element.62, ...), kind=kOutput, calls=%fused_computation.9 | convolution fusion | flops 806486016 | bytes 4205584 | tf_op jit(solution)/shard_map/dot_general | solution.py:28
  123.2 4.6 %fusion.2 = f32[8,256,256]{2,1,0:T(8,128)S(1)} fusion(f32[4,8,64,256,1]{3,2,4,0,1:T(8,128)S(1)} %fusion, f32[]{:T(128)S(6)} %mul.657, f32[256,256]{1,0:T(8,128)S(1)} %copy.96, f32[8,256]{1,0:T(8,128)S(1)} %copy.94, f32[256]{0:T(256)S(1)} %get-tuple-element.50, f32[256]{0:T(256)S(1)} %get-tuple-element.51, f32[256]{0:T(256)S(1)} %get-tuple-element.52, ...), kind=kOutput, calls=%fused_computation.13 | convolution fusion | flops 808058880 | bytes 4475924 | tf_op jit(solution)/shard_map/dot_general | solution.py:28
  127.8 2.4 %copy.101 = f32[256,2,8,128]{3,1,2,0:T(2,128)} copy(f32[256,2,8,128]{3,2,1,0:T(8,128)S(1)} %bitcast.93) | data formatting | bytes 4194304
  (53 shorter events, 13.4 us)
Async XLA Ops:
  3.7 11.5 %copy-start.1 = (f32[2,16]{1,0:T(2,128)S(1)}, f32[2,16]{1,0:T(2,128)}, u32[]{:S(2)}) copy-start(f32[2,16]{1,0:T(2,128)} %param.3) | copy-start | bytes 388
  3.7 41.1 %all-to-all-start = ((f32[128,2,8,256]{3,2,1,0:T(8,128)}), f32[128,2,8,256]{3,2,1,0:T(8,128)S(1)}, u32[]{:S(2)}, u32[]{:S(2)}) async-start(f32[128,2,8,256]{3,2,1,0:T(8,128)} %copy.82), calls=%async_computation | async-start | bytes 4194304 | tf_op jit(solution)/shard_map/all_to_all | solution.py:68
  59.8 3.0 %copy-start = (f32[128,32,128]{2,1,0:T(8,128)S(1)}, f32[128,32,128]{2,1,0:T(8,128)}, u32[]{:S(2)}) copy-start(f32[128,32,128]{2,1,0:T(8,128)} %reshape.668) | copy-start | bytes 6291460
  64.5 41.6 %all-to-all-start.1 = ((f32[128,33,128]{2,1,0:T(8,128)}), f32[128,33,128]{2,1,0:T(8,128)S(1)}, u32[]{:S(2)}, u32[]{:S(2)}) async-start(f32[128,33,128]{2,1,0:T(8,128)} %pad_maximum_fusion), calls=%async_computation.1 | async-start | bytes 5242880 | tf_op jit(solution)/shard_map/all_to_all | solution.py:93

commit v6 on v5

--- a/solution.py
+++ b/solution.py
@@ -67,9 +67,10 @@
     sending = jnp.transpose(state.reshape(2, spread, -1, LANES), (3, 0, 2, 1))
     received = lax.all_to_all(sending, AXES, 0, 0, tiled=True)
     kernel1 = kernel1 * bond1[me % 4, column // quarter][None, :]
+    kernel1 = kernel1.reshape(spread, quarter, 4).transpose(0, 2, 1).reshape(spread, spread)
     current = dot(kernel1, received.reshape(spread, -1, spread), (0,), (0,), BLOCK_PRECISION)
     current = dot(current.reshape(-1, spread), kernel2, (1,), (0,), BLOCK_PRECISION)
-    pattern2 = bond2[column % 4][:, column // quarter]
+    pattern2 = bond2[column // quarter][:, column // quarter]
     current = current.reshape(spread, -1, spread) * pattern2[:, None, :]
     current = jnp.transpose(current, (1, 0, 2))
 
@@ -80,13 +81,14 @@
     rows = lax.dynamic_slice_in_dim(kernel3.reshape(per, devices // 4, spread), me // 4, 1, axis=1)
     cols = lax.dynamic_slice_in_dim(gather, (me % 4) * quarter, quarter, axis=1)
     weight = dot(rows.reshape(per, spread), cols.reshape(spread, -1), (1,), (0,))
-    weight = weight.reshape(per, quarter, 1, 4)
+    weight = weight.reshape(per, 1, quarter, 4)
     selector = (column[:, None] % 4 == jnp.arange(4)[None, :]).astype(jnp.float32)
     marginal = dot(current.reshape(-1, spread), selector, (1,), (0,))
     middle_part = jnp.sum(marginal)
-    final_part = jnp.sum(marginal.reshape(per, quarter, 4, 4) * weight)
+    final_part = jnp.sum(marginal.reshape(per, 4, quarter, 4) * weight)
 
-    sending = current.reshape(per * quarter, -1).T.reshape(devices, -1, LANES)
+    sending = jnp.transpose(current.reshape(per, 4, quarter, spread), (1, 3, 0, 2))
+    sending = sending.reshape(devices, -1, LANES)
     lane = jnp.arange(LANES, dtype=jnp.int32)
     extra = jnp.where(lane == 0, middle_part, jnp.where(lane == 1, final_part, 0.0))
     extra = jnp.broadcast_to(extra[None, None, :], (devices, 1, LANES))

time: 132 us -> 133 us (level)
    reshape x3 -> x2, local copies, waits for them, and re-layouts: 7.17 us -> 7.38 us  [the longest x1 4.61 us: shards(): sending = sending.reshape(devices, -1, LANES)]
    add x8 -> x10, other arithmetic: 9.62 us -> 9.6 us  [block_kernel(): kernel = kernel * (1.0 + horizontal[level] * chained)[None, :]]
where the time goes in v6:
time: 133 us; the launch traced here: 132 us
  waiting for transfers between devices  32.4 us (24%)
  local copies, waits for them, and re-layouts  31.2 us (23%)
  matrix products  24.4 us (18%)
  other arithmetic  21.4 us (16%)
  starting transfers between devices  18.3 us (14%)
  between operations  4.28 us (3%)
    all_to_all x1, waiting for transfers between devices, shards(): lax.all_to_all(jnp.concatenate([sending, extra], axis=1), AXES, 0, 0, til...  29.5 us
    dot_general x7, matrix products, dot(): lax.dot_general(lhs, rhs, ((lhs_dims, rhs_dims), ((), ())), precision=pre...  24.4 us
    all_to_all x1, starting transfers between devices, shards(): received = lax.all_to_all(sending, AXES, 0, 0, tiled=True)  11.5 us
    add x10, other arithmetic, block_kernel(): kernel = kernel * (1.0 + horizontal[level] * chained)[None, :]  9.6 us
    all_to_all x1, starting transfers between devices, shards(): lax.all_to_all(jnp.concatenate([sending, extra], axis=1), AXES, 0, 0, til...  6.83 us
    reshape x1, local copies, waits for them, and re-layouts, shards(): sending = sending.reshape(devices, -1, LANES)  4.61 us
    reshape x1, local copies, waits for them, and re-layouts, shards(): current = received.reshape(devices // 4, 4, 8, per, quarter)  4.36 us
    transpose x1, local copies, waits for them, and re-layouts, shards(): sending = jnp.transpose(state.reshape(2, spread, -1, LANES), (3, 0, 2, 1))  3.11 us
  transfers between devices with their start and end apart: 2, of which 2 were waited for; matrix products, arithmetic and copies ran while one was open for 24% of the time, Pallas kernels for 0%

profile of v6, /device:TPU:1, one launch (start us, length us, event | category | flops | bytes accessed | tf_op | source)
XLA Modules:
  0.0 132.0 jit_solution(8367090790009671598)
XLA Ops:
  0.6 3.1 %copy.88 = f32[128,2,8,256]{3,2,1,0:T(8,128)} copy(f32[128,2,8,256]{0,2,3,1:T(8,128)} %bitcast.95) | data formatting | bytes 4194304 | tf_op jit(solution)/shard_map/transpose | solution.py:67
  3.7 11.5 %all-to-all-start = ((f32[128,2,8,256]{3,2,1,0:T(8,128)}), f32[128,2,8,256]{3,2,1,0:T(8,128)S(1)}, u32[]{:S(2)}, u32[]{:S(2)}) async-start(f32[128,2,8,256]{3,2,1,0:T(8,128)} %copy.88), calls=%async_computation | async-start | bytes 4194304 | tf_op jit(solution)/shard_map/all_to_all | solution.py:68
  19.0 1.3 select_add_fusion.11
  21.8 1.3 %select_add_fusion.3 = (f32[4,64]{1,0:T(4,128)S(1)}, f32[4,64]{1,0:T(4,128)S(1)}) fusion(f32[]{:T(128)} %bitcast.45, f32[]{:T(128)} %bitcast.44), kind=kLoop, calls=%fused_computation.287 | loop fusion | flops 12288 | bytes 2056 | tf_op jit(solution)/shard_map/add | solution.py:21
  23.1 2.8 %multiply_reduce_fusion = f32[256,4]{0,1:T(4,128)S(1)} fusion(f32[4,64]{1,0:T(4,128)S(1)} %get-tuple-element.49, f32[4,64]{1,0:T(4,128)S(1)} %get-tuple-element.50, f32[4,64]{1,0:T(4,128)S(1)} %select_add_fusion.5, f32[]{:T(128)} %bitcast.42, s32[4,64]{1,0:T(4,128)S(1)} %get-tuple-element.45, s32[256]{0:T(256)S(1)} %get-tuple-element.54, f32[]{:T(128)} %bitcast.41, ...), kind=kLoop, calls=%fused_computation.54 | loop fusion | flops 1244160 | bytes 15376 | tf_op jit(solution)/shard_map/reduce_sum | solution.py:77
  25.9 0.8 fusion.217
  26.7 1.0 gather_fusion.4
  27.8 1.3 select_add_fusion.13
  29.7 2.4 %gather_fusion = f32[256]{0:T(256)S(1)} fusion(f32[4,4]{1,0:T(4,128)S(1)} %select_add_fusion.8, s32[256]{0:T(256)S(1)} %bitcast.93), kind=kCustom, calls=%fused_computation | custom fusion | bytes 4096 | tf_op jit(solution)/shard_map/gather | solution.py:69
  32.4 0.7 gather_fusion.1
  33.5 0.8 compare_select_fusion
  35.8 1.0 fusion.11
  36.9 1.0 gather_fusion.2
  38.7 1.3 %select_add_fusion.15 = (f32[256]{0:T(256)S(1)}, f32[256]{0:T(256)S(1)}) fusion(f32[]{:T(128)} %bitcast.20, f32[]{:T(128)} %bitcast.19), kind=kLoop, calls=%fused_computation.362 | loop fusion | flops 11776 | bytes 2056 | tf_op jit(solution)/shard_map/add | solution.py:21
  41.8 3.0 %all-to-all-done = f32[128,2,8,256]{3,2,1,0:T(8,128)S(1)} async-done(((f32[128,2,8,256]{3,2,1,0:T(8,128)}), f32[128,2,8,256]{3,2,1,0:T(8,128)S(1)}, u32[]{:S(2)}, u32[]{:S(2)}) %all-to-all-start) | async-done | bytes 2097184 | tf_op jit(solution)/shard_map/all_to_all | solution.py:68
  44.8 4.3 %fusion.4 = f32[256,8,256]{2,0,1:T(8,128)S(1)} fusion(f32[256,8,256]{2,1,0:T(8,128)S(1)} %bitcast.94, f32[256]{0:T(256)S(1)} %mul.554, f32[256]{0:T(256)S(1)} %fusion.209, f32[256]{0:T(256)S(1)} %get-tuple-element.9, f32[256]{0:T(256)S(1)} %get-tuple-element.6, f32[]{:T(128)} %bitcast.3, s32[256]{0:T(256)S(1)} %get-tuple-element.53, f32[]{:T(128)} %bitcast.2, ...), kind=kOutput, calls=%fused_computation.16 | convolution fusion | flops 806551552 | bytes 4206608 | tf_op jit(solution)/shard_map/dot_general | solution.py:28
  49.2 3.7 %convolution_multiply_fusion = f32[256,8,256]{2,0,1:T(8,128)S(1)} fusion(f32[256,8,256]{2,0,1:T(8,128)S(1)} %fusion.4, f32[256,256]{1,0:T(8,128)S(1)} %copy.92, f32[256]{0:T(256)S(1)} %get-tuple-element.63, f32[256]{0:T(256)S(1)} %get-tuple-element.64, f32[256]{0:T(256)S(1)} %select_add_fusion.17, f32[]{:T(128)} %bitcast.17, s32[256]{0:T(256)S(1)} %get-tuple-element.54, ...), kind=kOutput, calls=%fused_computation.18 | convolution fusion | flops 807010304 | bytes 4463632 | tf_op jit(solution)/shard_map/dot_general | solution.py:28
  52.9 2.8 %copy.93 = f32[8,4,64,256]{2,0,3,1:T(8,128)} copy(f32[8,4,64,256]{3,2,1,0:T(8,128)S(1)} %bitcast.90) | data formatting | bytes 4194304 | tf_op jit(solution)/shard_map/reshape | solution.py:90
  55.6 4.6 %reshape.790 = f32[128,32,128]{2,1,0:T(8,128)} reshape(f32[4,256,8,64]{3,2,1,0:T(8,128)} %bitcast.92) | data formatting | bytes 4194304 | tf_op jit(solution)/shard_map/reshape | solution.py:91
  60.2 1.7 %fusion.234 = (f32[]{:T(128)}, f32[]{:T(128)}) fusion(f32[2048,4]{0,1:T(4,128)S(1)} %mul.640, f32[2048,256]{1,0:T(8,128)S(1)} %bitcast.91, s32[256]{0:T(256)S(1)} %get-tuple-element.54), kind=kOutput, calls=%fused_computation.383 | convolution fusion | flops 25191422 | bytes 2130952 | tf_op jit(solution)/shard_map/dot_general | solution.py:28
  62.0 1.3 compare_select_fusion.17
  63.3 1.7 %pad_maximum_fusion = f32[128,33,128]{2,1,0:T(8,128)} fusion(f32[128,1,128]{2,1,0:T(1,128)S(1)} %broadcast_in_dim.14, f32[128,32,128]{2,1,0:T(8,128)S(1)} %copy-done), kind=kLoop, calls=%fused_computation.11 | loop fusion | flops 540672 | bytes 4325376 | tf_op jit(solution)/shard_map/concatenate | solution.py:95
  65.0 6.8 %all-to-all-start.1 = ((f32[128,33,128]{2,1,0:T(8,128)}), f32[128,33,128]{2,1,0:T(8,128)S(1)}, u32[]{:S(2)}, u32[]{:S(2)}) async-start(f32[128,33,128]{2,1,0:T(8,128)} %pad_maximum_fusion), calls=%async_computation.1 | async-start | bytes 5242880 | tf_op jit(solution)/shard_map/all_to_all | solution.py:95
  74.8 1.0 gather_fusion.8
  75.9 1.3 select_add_fusion.9
  77.3 29.5 %all-to-all-done.1 = f32[128,33,128]{2,1,0:T(8,128)S(1)} async-done(((f32[128,33,128]{2,1,0:T(8,128)}), f32[128,33,128]{2,1,0:T(8,128)S(1)}, u32[]{:S(2)}, u32[]{:S(2)}) %all-to-all-start.1) | async-done | bytes 2162720 | tf_op jit(solution)/shard_map/all_to_all | solution.py:95
  106.8 0.8 slice_reduce_fusion
  109.6 1.6 %slice.230 = f32[128,32,128]{2,1,0:T(8,128)} slice(f32[128,33,128]{2,1,0:T(8,128)S(1)} %all-to-all-done.1), slice={[0:128], [0:32], [0:128]} | slice | bytes 4194304 | tf_op jit(solution)/shard_map/slice | solution.py:98
  111.2 4.4 %reshape.795 = f32[32,4,8,8,64]{4,3,2,1,0:T(8,128)} reshape(f32[128,32,128]{2,1,0:T(8,128)} %slice.230) | data formatting | bytes 4194304 | tf_op jit(solution)/shard_map/reshape | solution.py:99
  115.6 8.3 %fusion = f32[4,8,64,256,1]{3,2,4,0,1:T(8,128)S(1)} fusion(f32[32,4,8,8,64]{4,3,2,1,0:T(8,128)} %reshape.795, f32[256]{0:T(256)S(1)} %get-tuple-element.60, f32[256]{0:T(256)S(1)} %get-tuple-element.61, f32[256]{0:T(256)S(1)} %get-tuple-element.62, f32[]{:T(128)} %bitcast.32, s32[256]{0:T(256)S(1)} %get-tuple-element.54, s32[32,8]{1,0:T(8,128)S(1)} %get-tuple-element.65, ...), kind=kOutput, calls=%fused_computation.9 | convolution fusion | flops 806486016 | bytes 4205584 | tf_op jit(solution)/shard_map/dot_general | solution.py:28
  123.9 4.6 %fusion.2 = f32[8,256,256]{2,1,0:T(8,128)S(1)} fusion(f32[4,8,64,256,1]{3,2,4,0,1:T(8,128)S(1)} %fusion, f32[]{:T(128)S(6)} %mul.687, f32[256,256]{1,0:T(8,128)S(1)} %copy.102, f32[8,256]{1,0:T(8,128)S(1)} %copy.100, f32[256]{0:T(256)S(1)} %get-tuple-element.57, f32[256]{0:T(256)S(1)} %get-tuple-element.58, f32[256]{0:T(256)S(1)} %get-tuple-element.59, ...), kind=kOutput, calls=%fused_computation.13 | convolution fusion | flops 808058880 | bytes 4475924 | tf_op jit(solution)/shard_map/dot_general | solution.py:28
  128.5 2.4 %copy.107 = f32[256,2,8,128]{3,1,2,0:T(2,128)} copy(f32[256,2,8,128]{3,2,1,0:T(8,128)S(1)} %bitcast.96) | data formatting | bytes 4194304
  (71 shorter events, 13.7 us)
Async XLA Ops:
  3.7 11.7 %copy-start.1 = (f32[2,16]{1,0:T(2,128)S(1)}, f32[2,16]{1,0:T(2,128)}, u32[]{:S(2)}) copy-start(f32[2,16]{1,0:T(2,128)} %param.3) | copy-start | bytes 388
  3.7 41.1 %all-to-all-start = ((f32[128,2,8,256]{3,2,1,0:T(8,128)}), f32[128,2,8,256]{3,2,1,0:T(8,128)S(1)}, u32[]{:S(2)}, u32[]{:S(2)}) async-start(f32[128,2,8,256]{3,2,1,0:T(8,128)} %copy.88), calls=%async_computation | async-start | bytes 4194304 | tf_op jit(solution)/shard_map/all_to_all | solution.py:68
  60.2 3.1 %copy-start = (f32[128,32,128]{2,1,0:T(8,128)S(1)}, f32[128,32,128]{2,1,0:T(8,128)}, u32[]{:S(2)}) copy-start(f32[128,32,128]{2,1,0:T(8,128)} %reshape.790) | copy-start | bytes 6291460
  65.0 41.7 %all-to-all-start.1 = ((f32[128,33,128]{2,1,0:T(8,128)}), f32[128,33,128]{2,1,0:T(8,128)S(1)}, u32[]{:S(2)}, u32[]{:S(2)}) async-start(f32[128,33,128]{2,1,0:T(8,128)} %pad_maximum_fusion), calls=%async_computation.1 | async-start | bytes 5242880 | tf_op jit(solution)/shard_map/all_to_all | solution.py:95

commit v7 on v5

--- a/solution.py
+++ b/solution.py
@@ -90,7 +90,10 @@
     lane = jnp.arange(LANES, dtype=jnp.int32)
     extra = jnp.where(lane == 0, middle_part, jnp.where(lane == 1, final_part, 0.0))
     extra = jnp.broadcast_to(extra[None, None, :], (devices, 1, LANES))
-    received = lax.all_to_all(jnp.concatenate([sending, extra], axis=1), AXES, 0, 0, tiled=True)
+    payload = jnp.concatenate([sending, extra], axis=1)
+    lead_part = payload.reshape(lead_count, sub_count, -1, LANES)
+    lead_part = lax.all_to_all(lead_part, "sub", 1, 1, tiled=True)
+    received = lax.all_to_all(lead_part, "lead", 0, 0, tiled=True).reshape(devices, -1, LANES)
     middle_total = jnp.sum(received[:, -1, 0])
     final_total = jnp.sum(received[:, -1, 1])
     received = received[:, :-1, :]

time: 132 us -> 161 us (1.22)
  blocking collectives: 0 us -> 31.1 us
  waiting for transfers between devices: 32.6 us -> 25 us
  local copies, waits for them, and re-layouts: 31 us -> 37.8 us
    all_to_all x0 -> x1, blocking collectives: none -> 31.1 us  [shards(): lead_part = lax.all_to_all(lead_part, 'sub', 1, 1, tiled=True)]
    all_to_all x1, waiting for transfers between devices: 29.5 us -> 22.2 us  [shards(): lax.all_to_all(lead_part, 'lead', 0, 0, tiled=True)]
    all_to_all x0 -> x2, local copies, waits for them, and re-layouts: none -> 4.94 us  [the longest x1 2.74 us: shards(): lead_part = lax.all_to_all(lead_part, 'sub', 1, 1, tiled=True)]
    concatenate x0 -> x2, local copies, waits for them, and re-layouts: none -> 3.86 us  [shards(): payload = jnp.concatenate([sending, extra], axis=1)]
    slice x1 -> x2, local copies, waits for them, and re-layouts: 1.61 us -> 4.27 us  [shards(): received = received[:, :-1, :]]
    reshape x3 -> x2, local copies, waits for them, and re-layouts: 7.17 us -> 4.56 us  [shards(): sending = current.reshape(per * quarter, -1).T.reshape(devices, -1, LANES)]
    reshape x1, local copies, waits for them, and re-layouts: 4.35 us -> 2.31 us  [shards(): current = received.reshape(devices // 4, 4, 8, per, quarter)]
  transfers between devices with their start and end apart: 2 -> 2, of which waited for: 2 -> 2; matrix products, arithmetic and copies ran while one was open for 24% -> 20% of each run, Pallas kernels for 0% -> 0%
where the time goes in v7:
time: 161 us; the launch traced here: 159 us
  local copies, waits for them, and re-layouts  37.8 us (23%)
  blocking collectives  31.1 us (19%)
  waiting for transfers between devices  25 us (16%)
  matrix products  24.5 us (15%)
  other arithmetic  19.8 us (12%)
  starting transfers between devices  16.8 us (10%)
  between operations  4.27 us (3%)
    all_to_all x1, blocking collectives, shards(): lead_part = lax.all_to_all(lead_part, 'sub', 1, 1, tiled=True)  31.1 us
    dot_general x7, matrix products, dot(): lax.dot_general(lhs, rhs, ((lhs_dims, rhs_dims), ((), ())), precision=pre...  24.5 us
    all_to_all x1, waiting for transfers between devices, shards(): lax.all_to_all(lead_part, 'lead', 0, 0, tiled=True)  22.2 us
    all_to_all x1, starting transfers between devices, shards(): received = lax.all_to_all(sending, AXES, 0, 0, tiled=True)  11.5 us
    add x8, other arithmetic, block_kernel(): kernel = kernel * (1.0 + horizontal[level] * chained)[None, :]  9.51 us
    all_to_all x1, starting transfers between devices, shards(): lax.all_to_all(lead_part, 'lead', 0, 0, tiled=True)  5.35 us
    reshape x2, local copies, waits for them, and re-layouts, shards(): sending = current.reshape(per * quarter, -1).T.reshape(devices, -1, LANES)  4.56 us
    slice x2, local copies, waits for them, and re-layouts, shards(): received = received[:, :-1, :]  4.27 us
  transfers between devices with their start and end apart: 2, of which 2 were waited for; matrix products, arithmetic and copies ran while one was open for 20% of the time, Pallas kernels for 0%

profile of v7, /device:TPU:1, one launch (start us, length us, event | category | flops | bytes accessed | tf_op | source)
XLA Modules:
  0.0 159.3 jit_solution(10694928913923952328)
XLA Ops:
  0.6 3.1 %copy.108 = f32[128,2,8,256]{3,2,1,0:T(8,128)} copy(f32[128,2,8,256]{0,2,3,1:T(8,128)} %bitcast.95) | data formatting | bytes 4194304 | tf_op jit(solution)/shard_map/transpose | solution.py:67
  3.7 11.5 %all-to-all-start = ((f32[128,2,8,256]{3,2,1,0:T(8,128)}), f32[128,2,8,256]{3,2,1,0:T(8,128)S(1)}, u32[]{:S(2)}, u32[]{:S(2)}) async-start(f32[128,2,8,256]{3,2,1,0:T(8,128)} %copy.108), calls=%async_computation | async-start | bytes 4194304 | tf_op jit(solution)/shard_map/all_to_all | solution.py:68
  18.1 1.3 select_add_fusion.3
  19.4 2.9 %multiply_reduce_fusion = f32[256,4]{0,1:T(4,128)S(1)} fusion(f32[4,64]{1,0:T(4,128)S(1)} %get-tuple-element.44, f32[4,64]{1,0:T(4,128)S(1)} %get-tuple-element.45, f32[4,64]{1,0:T(4,128)S(1)} %select_add_fusion.5, f32[]{:T(128)} %bitcast.41, s32[4,64]{1,0:T(4,128)S(1)} %get-tuple-element.40, s32[256]{0:T(256)S(1)} %get-tuple-element.46, f32[]{:T(128)} %bitcast.40, ...), kind=kLoop, calls=%fused_computation.83 | loop fusion | flops 1244160 | bytes 15376 | tf_op jit(solution)/shard_map/reduce_sum | solution.py:76
  25.8 1.2 select_add_fusion.11
  27.1 1.4 select_add_fusion.13
  32.9 1.1 fusion.40
  35.8 2.4 %gather_fusion = f32[256]{0:T(256)S(1)} fusion(f32[4,4]{1,0:T(4,128)S(1)} %select_add_fusion.8, s32[256]{0:T(256)S(1)} %bitcast.90), kind=kCustom, calls=%fused_computation | custom fusion | bytes 4096 | tf_op jit(solution)/shard_map/gather | solution.py:69
  38.2 1.3 select_add_fusion.17
  39.5 1.2 select_add_fusion.19
  40.7 1.3 select_add_fusion.15
  42.0 2.8 %all-to-all-done = f32[128,2,8,256]{3,2,1,0:T(8,128)S(1)} async-done(((f32[128,2,8,256]{3,2,1,0:T(8,128)}), f32[128,2,8,256]{3,2,1,0:T(8,128)S(1)}, u32[]{:S(2)}, u32[]{:S(2)}) %all-to-all-start) | async-done | bytes 2097184 | tf_op jit(solution)/shard_map/all_to_all | solution.py:68
  44.8 4.2 %fusion.4 = f32[256,8,256]{2,0,1:T(8,128)S(1)} fusion(f32[256,8,256]{2,1,0:T(8,128)S(1)} %bitcast.93, f32[256]{0:T(256)S(1)} %gather_fusion, f32[256]{0:T(256)S(1)} %get-tuple-element.59, f32[256]{0:T(256)S(1)} %get-tuple-element.60, f32[256]{0:T(256)S(1)} %get-tuple-element.61, f32[]{:T(128)} %bitcast.3, s32[256]{0:T(256)S(1)} %get-tuple-element.46, ...), kind=kOutput, calls=%fused_computation.16 | convolution fusion | flops 806551552 | bytes 4202512 | tf_op jit(solution)/shard_map/dot_general | solution.py:28
  49.0 3.7 %convolution_multiply_fusion = f32[256,8,256]{2,0,1:T(8,128)S(1)} fusion(f32[256,8,256]{2,0,1:T(8,128)S(1)} %fusion.4, f32[256,256]{1,0:T(8,128)S(1)} %copy.112, f32[256]{0:T(256)S(1)} %get-tuple-element.56, f32[256]{0:T(256)S(1)} %get-tuple-element.57, f32[256]{0:T(256)S(1)} %get-tuple-element.58, f32[]{:T(128)} %bitcast.16, f32[]{:T(128)} %bitcast.15, ...), kind=kOutput, calls=%fused_computation.18 | convolution fusion | flops 807010304 | bytes 4463632 | tf_op jit(solution)/shard_map/dot_general | solution.py:28
  52.7 1.6 %reshape.672 = f32[512,1024]{1,0:T(8,128)} reshape(f32[8,256,256]{2,1,0:T(8,128)S(1)} %bitcast.88) | data formatting | bytes 4194304 | tf_op jit(solution)/shard_map/reshape | solution.py:89
  54.3 2.9 %copy.113 = f32[512,1024]{0,1:T(8,128)} copy(f32[512,1024]{1,0:T(8,128)} %reshape.672) | data formatting | bytes 4194304 | tf_op jit(solution)/shard_map/reshape | solution.py:89
  57.3 2.6 %concatenate.10 = f32[32,4,32,128]{3,2,1,0:T(8,128)} reshape(f32[1024,512]{1,0:T(8,128)} %bitcast.94) | data formatting | bytes 4194304 | tf_op jit(solution)/shard_map/concatenate | solution.py:93
  59.9 1.7 %fusion.216 = (f32[]{:T(128)}, f32[]{:T(128)}) fusion(f32[2048,4]{0,1:T(4,128)S(1)} %mul.610, f32[2048,256]{1,0:T(8,128)S(1)} %bitcast.89, s32[256]{0:T(256)S(1)} %get-tuple-element.46), kind=kOutput, calls=%fused_computation.347 | convolution fusion | flops 25191422 | bytes 2130952 | tf_op jit(solution)/shard_map/dot_general | solution.py:28
  61.6 1.3 compare_select_fusion.19
  63.2 1.3 copy.118
  64.5 31.1 %all_to_all.15 = f32[32,4,33,128]{3,0,2,1:T(8,128)S(1)} all-to-all(f32[32,4,33,128]{3,0,2,1:T(8,128)S(1)} %copy.118), channel_id=1, replica_groups=mesh['lead'=32,'sub'=4] {'sub'}, dimensions={1} | all-to-all | bytes 4325376 | tf_op jit(solution)/shard_map/all_to_all | solution.py:95
  95.5 2.7 %copy.119 = f32[32,4,33,128]{3,1,2,0:T(4,128)} copy(f32[32,4,33,128]{3,0,2,1:T(8,128)S(1)} %all_to_all.15) | data formatting | bytes 4325376 | tf_op jit(solution)/shard_map/all_to_all | solution.py:95
  98.3 5.3 %all-to-all-start.2 = ((f32[32,4,33,128]{3,1,2,0:T(4,128)}), f32[32,4,33,128]{3,1,2,0:T(4,128)}, u32[]{:S(2)}, u32[]{:S(2)}) async-start(f32[32,4,33,128]{3,1,2,0:T(4,128)} %copy.119), calls=%async_computation.2 | async-start | bytes 4325376 | tf_op jit(solution)/shard_map/all_to_all | solution.py:96
  107.7 1.3 select_add_fusion.9
  109.0 22.2 %all-to-all-done.2 = f32[32,4,33,128]{3,1,2,0:T(4,128)} async-done(((f32[32,4,33,128]{3,1,2,0:T(4,128)}), f32[32,4,33,128]{3,1,2,0:T(4,128)}, u32[]{:S(2)}, u32[]{:S(2)}) %all-to-all-start.2) | async-done | bytes 2162720 | tf_op jit(solution)/shard_map/all_to_all | solution.py:96
  131.3 2.2 %copy.120 = f32[32,4,33,128]{3,1,0,2:T(4,128)S(1)} copy(f32[32,4,33,128]{3,1,2,0:T(4,128)} %all-to-all-done.2) | data formatting | bytes 4325376 | tf_op jit(solution)/shard_map/all_to_all | solution.py:96
  136.2 1.5 slice.230
  137.7 2.8 %copy.121 = f32[128,32,128]{2,1,0:T(8,128)S(1)} copy(f32[128,32,128]{2,0,1:T(8,128)} %slice.230) | data formatting | bytes 4194304 | tf_op jit(solution)/shard_map/slice | solution.py:99
  140.5 2.3 %reshape.678 = f32[32,4,8,8,64]{4,3,2,1,0:T(8,128)} reshape(f32[128,32,128]{2,1,0:T(8,128)S(1)} %copy.121) | data formatting | bytes 4194304 | tf_op jit(solution)/shard_map/reshape | solution.py:100
  142.8 8.4 %fusion = f32[4,8,64,256,1]{3,2,4,0,1:T(8,128)S(1)} fusion(f32[32,4,8,8,64]{4,3,2,1,0:T(8,128)} %reshape.678, f32[256]{0:T(256)S(1)} %get-tuple-element.53, f32[256]{0:T(256)S(1)} %get-tuple-element.54, f32[256]{0:T(256)S(1)} %get-tuple-element.55, f32[]{:T(128)} %bitcast.31, s32[256]{0:T(256)S(1)} %get-tuple-element.46, s32[32,8]{1,0:T(8,128)S(1)} %get-tuple-element.62, ...), kind=kOutput, calls=%fused_computation.9 | convolution fusion | flops 806486016 | bytes 4205584 | tf_op jit(solution)/shard_map/dot_general | solution.py:28
  151.2 4.6 %fusion.2 = f32[8,256,256]{2,1,0:T(8,128)S(1)} fusion(f32[4,8,64,256,1]{3,2,4,0,1:T(8,128)S(1)} %fusion, f32[]{:T(128)S(6)} %mul.657, f32[256,256]{1,0:T(8,128)S(1)} %copy.126, f32[8,256]{1,0:T(8,128)S(1)} %copy.124, f32[256]{0:T(256)S(1)} %get-tuple-element.50, f32[256]{0:T(256)S(1)} %get-tuple-element.51, f32[256]{0:T(256)S(1)} %get-tuple-element.52, ...), kind=kOutput, calls=%fused_computation.13 | convolution fusion | flops 808058880 | bytes 4475924 | tf_op jit(solution)/shard_map/dot_general | solution.py:28
  155.8 2.4 %copy.131 = f32[256,2,8,128]{3,1,2,0:T(2,128)} copy(f32[256,2,8,128]{3,2,1,0:T(8,128)S(1)} %bitcast.96) | data formatting | bytes 4194304
  (58 shorter events, 17.5 us)
Async XLA Ops:
  3.7 11.5 %copy-start.1 = (f32[2,16]{1,0:T(2,128)S(1)}, f32[2,16]{1,0:T(2,128)}, u32[]{:S(2)}) copy-start(f32[2,16]{1,0:T(2,128)} %param.3) | copy-start | bytes 388
  3.7 41.1 %all-to-all-start = ((f32[128,2,8,256]{3,2,1,0:T(8,128)}), f32[128,2,8,256]{3,2,1,0:T(8,128)S(1)}, u32[]{:S(2)}, u32[]{:S(2)}) async-start(f32[128,2,8,256]{3,2,1,0:T(8,128)} %copy.108), calls=%async_computation | async-start | bytes 4194304 | tf_op jit(solution)/shard_map/all_to_all | solution.py:68
  59.9 3.0 %copy-start = (f32[32,4,32,128]{3,2,1,0:T(8,128)S(1)}, f32[32,4,32,128]{3,2,1,0:T(8,128)}, u32[]{:S(2)}) copy-start(f32[32,4,32,128]{3,2,1,0:T(8,128)} %concatenate.10) | copy-start | bytes 6291460
  98.3 33.0 %all-to-all-start.2 = ((f32[32,4,33,128]{3,1,2,0:T(4,128)}), f32[32,4,33,128]{3,1,2,0:T(4,128)}, u32[]{:S(2)}, u32[]{:S(2)}) async-start(f32[32,4,33,128]{3,1,2,0:T(4,128)} %copy.119), calls=%async_computation.2 | async-start | bytes 4325376 | tf_op jit(solution)/shard_map/all_to_all | solution.py:96

commit v8 on v5

--- a/solution.py
+++ b/solution.py
@@ -87,13 +87,13 @@
     final_part = jnp.sum(marginal.reshape(per, quarter, 4, 4) * weight)
 
     sending = current.reshape(per * quarter, -1).T.reshape(devices, -1, LANES)
-    lane = jnp.arange(LANES, dtype=jnp.int32)
-    extra = jnp.where(lane == 0, middle_part, jnp.where(lane == 1, final_part, 0.0))
-    extra = jnp.broadcast_to(extra[None, None, :], (devices, 1, LANES))
-    received = lax.all_to_all(jnp.concatenate([sending, extra], axis=1), AXES, 0, 0, tiled=True)
-    middle_total = jnp.sum(received[:, -1, 0])
-    final_total = jnp.sum(received[:, -1, 1])
-    received = received[:, :-1, :]
+    middle_row = jnp.broadcast_to(middle_part, (devices, 1, LANES))
+    final_row = jnp.broadcast_to(final_part, (devices, 1, LANES))
+    payload = jnp.concatenate([sending, middle_row, final_row], axis=1)
+    received = lax.all_to_all(payload, AXES, 0, 0, tiled=True)
+    middle_total = jnp.sum(received[:, -2, 0])
+    final_total = jnp.sum(received[:, -1, 0])
+    received = received[:, :-2, :]
     current = received.reshape(devices // 4, 4, 8, per, quarter)
     kernel3 = kernel3.reshape(per, devices // 4, spread).transpose(1, 0, 2)
     current = dot(current, kernel3, (0, 3), (0, 1), BLOCK_PRECISION)

time: 132 us -> 132 us (level)
    concatenate x0 -> x2, local copies, waits for them, and re-layouts: none -> 1.35 us  [shards(): payload = jnp.concatenate([sending, middle_row, final_row], axis=1)]
where the time goes in v8:
time: 132 us; the launch traced here: 131 us
  waiting for transfers between devices  32.6 us (25%)
  local copies, waits for them, and re-layouts  32.3 us (24%)
  matrix products  24.2 us (18%)
  other arithmetic  19.9 us (15%)
  starting transfers between devices  18.2 us (14%)
  between operations  4.22 us (3%)
    all_to_all x1, waiting for transfers between devices, shards(): received = lax.all_to_all(payload, AXES, 0, 0, tiled=True)  29.5 us
    dot_general x7, matrix products, dot(): lax.dot_general(lhs, rhs, ((lhs_dims, rhs_dims), ((), ())), precision=pre...  24.2 us
    all_to_all x1, starting transfers between devices, shards(): received = lax.all_to_all(sending, AXES, 0, 0, tiled=True)  11.5 us
    add x8, other arithmetic, block_kernel(): kernel = kernel * (1.0 + horizontal[level] * chained)[None, :]  9.62 us
    reshape x3, local copies, waits for them, and re-layouts, shards(): sending = current.reshape(per * quarter, -1).T.reshape(devices, -1, LANES)  7.17 us
    all_to_all x1, starting transfers between devices, shards(): received = lax.all_to_all(payload, AXES, 0, 0, tiled=True)  6.71 us
    reshape x1, local copies, waits for them, and re-layouts, shards(): current = received.reshape(devices // 4, 4, 8, per, quarter)  4.35 us
    transpose x1, local copies, waits for them, and re-layouts, shards(): sending = jnp.transpose(state.reshape(2, spread, -1, LANES), (3, 0, 2, 1))  3.11 us
  transfers between devices with their start and end apart: 2, of which 2 were waited for; matrix products, arithmetic and copies ran while one was open for 24% of the time, Pallas kernels for 0%

profile of v8, /device:TPU:1, one launch (start us, length us, event | category | flops | bytes accessed | tf_op | source)
XLA Modules:
  0.0 131.5 jit_solution(6800886760220755604)
XLA Ops:
  0.6 3.1 %copy.82 = f32[128,2,8,256]{3,2,1,0:T(8,128)} copy(f32[128,2,8,256]{0,2,3,1:T(8,128)} %bitcast.94) | data formatting | bytes 4194304 | tf_op jit(solution)/shard_map/transpose | solution.py:67
  3.7 11.5 %all-to-all-start = ((f32[128,2,8,256]{3,2,1,0:T(8,128)}), f32[128,2,8,256]{3,2,1,0:T(8,128)S(1)}, u32[]{:S(2)}, u32[]{:S(2)}) async-start(f32[128,2,8,256]{3,2,1,0:T(8,128)} %copy.82), calls=%async_computation | async-start | bytes 4194304 | tf_op jit(solution)/shard_map/all_to_all | solution.py:68
  18.1 1.3 select_add_fusion.3
  19.4 2.8 %multiply_reduce_fusion = f32[256,4]{0,1:T(4,128)S(1)} fusion(f32[4,64]{1,0:T(4,128)S(1)} %get-tuple-element.44, f32[4,64]{1,0:T(4,128)S(1)} %get-tuple-element.45, f32[4,64]{1,0:T(4,128)S(1)} %select_add_fusion.5, f32[]{:T(128)} %bitcast.41, s32[4,64]{1,0:T(4,128)S(1)} %get-tuple-element.40, s32[256]{0:T(256)S(1)} %get-tuple-element.46, f32[]{:T(128)} %bitcast.40, ...), kind=kLoop, calls=%fused_computation.83 | loop fusion | flops 1244160 | bytes 15376 | tf_op jit(solution)/shard_map/reduce_sum | solution.py:76
  23.0 1.0 gather_fusion.4
  25.6 1.4 %select_add_fusion.11 = (f32[256]{0:T(256)S(1)}, f32[256]{0:T(256)S(1)}) fusion(f32[]{:T(128)} %bitcast.42, f32[]{:T(128)} %bitcast.34), kind=kLoop, calls=%fused_computation.318 | loop fusion | flops 16128 | bytes 2056 | tf_op jit(solution)/shard_map/add | solution.py:21
  27.0 1.4 %select_add_fusion.13 = (f32[256]{0:T(256)S(1)}, f32[256]{0:T(256)S(1)}) fusion(f32[]{:T(128)} %bitcast.33, f32[]{:T(128)} %bitcast.32), kind=kLoop, calls=%fused_computation.320 | loop fusion | flops 15104 | bytes 2056 | tf_op jit(solution)/shard_map/add | solution.py:21
  29.2 1.0 gather_fusion.2
  32.1 0.8 select_add_fusion.1
  32.9 1.1 fusion.40
  35.7 2.4 %gather_fusion = f32[256]{0:T(256)S(1)} fusion(f32[4,4]{1,0:T(4,128)S(1)} %select_add_fusion.8, s32[256]{0:T(256)S(1)} %bitcast.91), kind=kCustom, calls=%fused_computation | custom fusion | bytes 4096 | tf_op jit(solution)/shard_map/gather | solution.py:69
  38.1 1.1 select_add_fusion.17
  39.2 1.3 select_add_fusion.19
  40.5 1.2 select_add_fusion.15
  41.7 3.1 %all-to-all-done = f32[128,2,8,256]{3,2,1,0:T(8,128)S(1)} async-done(((f32[128,2,8,256]{3,2,1,0:T(8,128)}), f32[128,2,8,256]{3,2,1,0:T(8,128)S(1)}, u32[]{:S(2)}, u32[]{:S(2)}) %all-to-all-start) | async-done | bytes 2097184 | tf_op jit(solution)/shard_map/all_to_all | solution.py:68
  44.8 4.2 %fusion.4 = f32[256,8,256]{2,0,1:T(8,128)S(1)} fusion(f32[256,8,256]{2,1,0:T(8,128)S(1)} %bitcast.92, f32[256]{0:T(256)S(1)} %gather_fusion, f32[256]{0:T(256)S(1)} %get-tuple-element.59, f32[256]{0:T(256)S(1)} %get-tuple-element.60, f32[256]{0:T(256)S(1)} %get-tuple-element.61, f32[]{:T(128)} %bitcast.3, s32[256]{0:T(256)S(1)} %get-tuple-element.46, ...), kind=kOutput, calls=%fused_computation.16 | convolution fusion | flops 806551552 | bytes 4202512 | tf_op jit(solution)/shard_map/dot_general | solution.py:28
  49.0 3.6 %convolution_multiply_fusion = f32[256,8,256]{2,0,1:T(8,128)S(1)} fusion(f32[256,8,256]{2,0,1:T(8,128)S(1)} %fusion.4, f32[256,256]{1,0:T(8,128)S(1)} %copy.86, f32[256]{0:T(256)S(1)} %get-tuple-element.56, f32[256]{0:T(256)S(1)} %get-tuple-element.57, f32[256]{0:T(256)S(1)} %get-tuple-element.58, f32[]{:T(128)} %bitcast.16, f32[]{:T(128)} %bitcast.15, ...), kind=kOutput, calls=%fused_computation.18 | convolution fusion | flops 807010304 | bytes 4463632 | tf_op jit(solution)/shard_map/dot_general | solution.py:28
  52.6 1.6 %reshape.657 = f32[512,1024]{1,0:T(8,128)} reshape(f32[8,256,256]{2,1,0:T(8,128)S(1)} %bitcast.89) | data formatting | bytes 4194304 | tf_op jit(solution)/shard_map/reshape | solution.py:89
  54.2 2.9 %copy.87 = f32[512,1024]{0,1:T(8,128)} copy(f32[512,1024]{1,0:T(8,128)} %reshape.657) | data formatting | bytes 4194304 | tf_op jit(solution)/shard_map/reshape | solution.py:89
  57.2 2.6 %reshape.658 = f32[128,32,128]{2,1,0:T(8,128)} reshape(f32[1024,512]{1,0:T(8,128)} %bitcast.93) | data formatting | bytes 4194304 | tf_op jit(solution)/shard_map/reshape | solution.py:89
  59.8 1.7 %fusion.216 = (f32[]{:T(128)}, f32[]{:T(128)}) fusion(f32[2048,4]{0,1:T(4,128)S(1)} %mul.610, f32[2048,256]{1,0:T(8,128)S(1)} %bitcast.90, s32[256]{0:T(256)S(1)} %get-tuple-element.46), kind=kOutput, calls=%fused_computation.345 | convolution fusion | flops 25191422 | bytes 2130952 | tf_op jit(solution)/shard_map/dot_general | solution.py:28
  62.8 1.8 %maximum_maximum_fusion = f32[128,34,128]{2,1,0:T(8,128)} fusion(f32[128,32,128]{2,1,0:T(8,128)S(1)} %copy-done, f32[34]{0:T(128)S(1)} %pad.3.clone, f32[34]{0:T(128)S(1)} %pad.2.clone), kind=kLoop, calls=%fused_computation.11 | loop fusion | flops 1114112 | bytes 4325648 | tf_op jit(solution)/shard_map/concatenate | solution.py:92
  64.6 6.7 %all-to-all-start.1 = ((f32[128,34,128]{2,1,0:T(8,128)}), f32[128,34,128]{2,1,0:T(8,128)S(1)}, u32[]{:S(2)}, u32[]{:S(2)}) async-start(f32[128,34,128]{2,1,0:T(8,128)} %maximum_maximum_fusion), calls=%async_computation.1 | async-start | bytes 5242880 | tf_op jit(solution)/shard_map/all_to_all | solution.py:93
  74.3 1.0 gather_fusion.8
  75.4 1.3 select_add_fusion.9
  76.7 29.5 %all-to-all-done.1 = f32[128,34,128]{2,1,0:T(8,128)S(1)} async-done(((f32[128,34,128]{2,1,0:T(8,128)}), f32[128,34,128]{2,1,0:T(8,128)S(1)}, u32[]{:S(2)}, u32[]{:S(2)}) %all-to-all-start.1) | async-done | bytes 2228256 | tf_op jit(solution)/shard_map/all_to_all | solution.py:93
  106.3 0.8 slice_reduce_fusion
  109.1 1.6 %slice.230 = f32[128,32,128]{2,1,0:T(8,128)} slice(f32[128,34,128]{2,1,0:T(8,128)S(1)} %all-to-all-done.1), slice={[0:128], [0:32], [0:128]} | slice | bytes 4194304 | tf_op jit(solution)/shard_map/slice | solution.py:96
  110.7 4.3 %reshape.663 = f32[32,4,8,8,64]{4,3,2,1,0:T(8,128)} reshape(f32[128,32,128]{2,1,0:T(8,128)} %slice.230) | data formatting | bytes 4194304 | tf_op jit(solution)/shard_map/reshape | solution.py:97
  115.1 8.3 %fusion = f32[4,8,64,256,1]{3,2,4,0,1:T(8,128)S(1)} fusion(f32[32,4,8,8,64]{4,3,2,1,0:T(8,128)} %reshape.663, f32[256]{0:T(256)S(1)} %get-tuple-element.53, f32[256]{0:T(256)S(1)} %get-tuple-element.54, f32[256]{0:T(256)S(1)} %get-tuple-element.55, f32[]{:T(128)} %bitcast.31, s32[256]{0:T(256)S(1)} %get-tuple-element.46, s32[32,8]{1,0:T(8,128)S(1)} %get-tuple-element.62, ...), kind=kOutput, calls=%fused_computation.9 | convolution fusion | flops 806486016 | bytes 4205584 | tf_op jit(solution)/shard_map/dot_general | solution.py:28
  123.4 4.6 %fusion.2 = f32[8,256,256]{2,1,0:T(8,128)S(1)} fusion(f32[4,8,64,256,1]{3,2,4,0,1:T(8,128)S(1)} %fusion, f32[]{:T(128)S(6)} %mul.657, f32[256,256]{1,0:T(8,128)S(1)} %copy.96, f32[8,256]{1,0:T(8,128)S(1)} %copy.94, f32[256]{0:T(256)S(1)} %get-tuple-element.50, f32[256]{0:T(256)S(1)} %get-tuple-element.51, f32[256]{0:T(256)S(1)} %get-tuple-element.52, ...), kind=kOutput, calls=%fused_computation.13 | convolution fusion | flops 808058880 | bytes 4475924 | tf_op jit(solution)/shard_map/dot_general | solution.py:28
  127.9 2.4 %copy.101 = f32[256,2,8,128]{3,1,2,0:T(2,128)} copy(f32[256,2,8,128]{3,2,1,0:T(8,128)S(1)} %bitcast.95) | data formatting | bytes 4194304
  (53 shorter events, 13.9 us)
Async XLA Ops:
  3.7 11.5 %copy-start.1 = (f32[2,16]{1,0:T(2,128)S(1)}, f32[2,16]{1,0:T(2,128)}, u32[]{:S(2)}) copy-start(f32[2,16]{1,0:T(2,128)} %param.3) | copy-start | bytes 388
  3.7 41.1 %all-to-all-start = ((f32[128,2,8,256]{3,2,1,0:T(8,128)}), f32[128,2,8,256]{3,2,1,0:T(8,128)S(1)}, u32[]{:S(2)}, u32[]{:S(2)}) async-start(f32[128,2,8,256]{3,2,1,0:T(8,128)} %copy.82), calls=%async_computation | async-start | bytes 4194304 | tf_op jit(solution)/shard_map/all_to_all | solution.py:68
  59.8 3.1 %copy-start = (f32[128,32,128]{2,1,0:T(8,128)S(1)}, f32[128,32,128]{2,1,0:T(8,128)}, u32[]{:S(2)}) copy-start(f32[128,32,128]{2,1,0:T(8,128)} %reshape.658) | copy-start | bytes 6291460
  64.6 41.6 %all-to-all-start.1 = ((f32[128,34,128]{2,1,0:T(8,128)}), f32[128,34,128]{2,1,0:T(8,128)S(1)}, u32[]{:S(2)}, u32[]{:S(2)}) async-start(f32[128,34,128]{2,1,0:T(8,128)} %maximum_maximum_fusion), calls=%async_computation.1 | async-start | bytes 5242880 | tf_op jit(solution)/shard_map/all_to_all | solution.py:93

commit v9 on v5

--- a/solution.py
+++ b/solution.py
@@ -82,7 +82,7 @@
     weight = dot(rows.reshape(per, spread), cols.reshape(spread, -1), (1,), (0,))
     weight = weight.reshape(per, quarter, 1, 4)
     selector = (column[:, None] % 4 == jnp.arange(4)[None, :]).astype(jnp.float32)
-    marginal = dot(current.reshape(-1, spread), selector, (1,), (0,))
+    marginal = dot(current.reshape(-1, spread), selector, (1,), (0,), BLOCK_PRECISION)
     middle_part = jnp.sum(marginal)
     final_part = jnp.sum(marginal.reshape(per, quarter, 4, 4) * weight)
 

time: 132 us -> 132 us (level)
  no operation moved by 1% of the time
where the time goes in v9:
time: 132 us; the launch traced here: 131 us
  waiting for transfers between devices  32.6 us (25%)
  local copies, waits for them, and re-layouts  31 us (23%)
  matrix products  23.9 us (18%)
  other arithmetic  21.1 us (16%)
  starting transfers between devices  18.2 us (14%)
  between operations  4.24 us (3%)
    all_to_all x1, waiting for transfers between devices, shards(): lax.all_to_all(jnp.concatenate([sending, extra], axis=1), AXES, 0, 0, til...  29.5 us
    dot_general x7, matrix products, dot(): lax.dot_general(lhs, rhs, ((lhs_dims, rhs_dims), ((), ())), precision=pre...  23.9 us
    all_to_all x1, starting transfers between devices, shards(): received = lax.all_to_all(sending, AXES, 0, 0, tiled=True)  11.5 us
    add x8, other arithmetic, block_kernel(): kernel = kernel * (1.0 + horizontal[level] * chained)[None, :]  9.62 us
    reshape x3, local copies, waits for them, and re-layouts, shards(): sending = current.reshape(per * quarter, -1).T.reshape(devices, -1, LANES)  7.17 us
    all_to_all x1, starting transfers between devices, shards(): lax.all_to_all(jnp.concatenate([sending, extra], axis=1), AXES, 0, 0, til...  6.71 us
    reshape x1, local copies, waits for them, and re-layouts, shards(): current = received.reshape(devices // 4, 4, 8, per, quarter)  4.35 us
    transpose x1, local copies, waits for them, and re-layouts, shards(): sending = jnp.transpose(state.reshape(2, spread, -1, LANES), (3, 0, 2, 1))  3.11 us
  transfers between devices with their start and end apart: 2, of which 2 were waited for; matrix products, arithmetic and copies ran while one was open for 24% of the time, Pallas kernels for 0%

profile of v9, /device:TPU:1, one launch (start us, length us, event | category | flops | bytes accessed | tf_op | source)
XLA Modules:
  0.0 131.0 jit_solution(2162822685216613356)
XLA Ops:
  0.6 3.1 %copy.82 = f32[128,2,8,256]{3,2,1,0:T(8,128)} copy(f32[128,2,8,256]{0,2,3,1:T(8,128)} %bitcast.92) | data formatting | bytes 4194304 | tf_op jit(solution)/shard_map/transpose | solution.py:67
  3.7 11.5 %all-to-all-start = ((f32[128,2,8,256]{3,2,1,0:T(8,128)}), f32[128,2,8,256]{3,2,1,0:T(8,128)S(1)}, u32[]{:S(2)}, u32[]{:S(2)}) async-start(f32[128,2,8,256]{3,2,1,0:T(8,128)} %copy.82), calls=%async_computation | async-start | bytes 4194304 | tf_op jit(solution)/shard_map/all_to_all | solution.py:68
  18.1 1.3 select_add_fusion.3
  19.4 2.8 %multiply_reduce_fusion = f32[256,4]{0,1:T(4,128)S(1)} fusion(f32[4,64]{1,0:T(4,128)S(1)} %get-tuple-element.44, f32[4,64]{1,0:T(4,128)S(1)} %get-tuple-element.45, f32[4,64]{1,0:T(4,128)S(1)} %select_add_fusion.5, f32[]{:T(128)} %bitcast.41, s32[4,64]{1,0:T(4,128)S(1)} %get-tuple-element.40, s32[256]{0:T(256)S(1)} %get-tuple-element.46, f32[]{:T(128)} %bitcast.40, ...), kind=kLoop, calls=%fused_computation.83 | loop fusion | flops 1244160 | bytes 15376 | tf_op jit(solution)/shard_map/reduce_sum | solution.py:76
  23.0 1.0 gather_fusion.4
  25.6 1.4 %select_add_fusion.11 = (f32[256]{0:T(256)S(1)}, f32[256]{0:T(256)S(1)}) fusion(f32[]{:T(128)} %bitcast.42, f32[]{:T(128)} %bitcast.34), kind=kLoop, calls=%fused_computation.320 | loop fusion | flops 16128 | bytes 2056 | tf_op jit(solution)/shard_map/add | solution.py:21
  27.0 1.4 %select_add_fusion.13 = (f32[256]{0:T(256)S(1)}, f32[256]{0:T(256)S(1)}) fusion(f32[]{:T(128)} %bitcast.33, f32[]{:T(128)} %bitcast.32), kind=kLoop, calls=%fused_computation.322 | loop fusion | flops 15104 | bytes 2056 | tf_op jit(solution)/shard_map/add | solution.py:21
  29.2 1.0 gather_fusion.2
  32.9 1.1 fusion.40
  35.7 2.4 %gather_fusion = f32[256]{0:T(256)S(1)} fusion(f32[4,4]{1,0:T(4,128)S(1)} %select_add_fusion.8, s32[256]{0:T(256)S(1)} %bitcast.89), kind=kCustom, calls=%fused_computation | custom fusion | bytes 4096 | tf_op jit(solution)/shard_map/gather | solution.py:69
  38.1 1.1 select_add_fusion.17
  39.2 1.3 select_add_fusion.19
  40.5 1.2 select_add_fusion.15
  41.7 3.1 %all-to-all-done = f32[128,2,8,256]{3,2,1,0:T(8,128)S(1)} async-done(((f32[128,2,8,256]{3,2,1,0:T(8,128)}), f32[128,2,8,256]{3,2,1,0:T(8,128)S(1)}, u32[]{:S(2)}, u32[]{:S(2)}) %all-to-all-start) | async-done | bytes 2097184 | tf_op jit(solution)/shard_map/all_to_all | solution.py:68
  44.8 4.2 %fusion.4 = f32[256,8,256]{2,0,1:T(8,128)S(1)} fusion(f32[256,8,256]{2,1,0:T(8,128)S(1)} %bitcast.90, f32[256]{0:T(256)S(1)} %gather_fusion, f32[256]{0:T(256)S(1)} %get-tuple-element.59, f32[256]{0:T(256)S(1)} %get-tuple-element.60, f32[256]{0:T(256)S(1)} %get-tuple-element.61, f32[]{:T(128)} %bitcast.3, s32[256]{0:T(256)S(1)} %get-tuple-element.46, ...), kind=kOutput, calls=%fused_computation.16 | convolution fusion | flops 806551552 | bytes 4202512 | tf_op jit(solution)/shard_map/dot_general | solution.py:28
  49.0 3.6 %convolution_multiply_fusion = f32[256,8,256]{2,0,1:T(8,128)S(1)} fusion(f32[256,8,256]{2,0,1:T(8,128)S(1)} %fusion.4, f32[256,256]{1,0:T(8,128)S(1)} %copy.86, f32[256]{0:T(256)S(1)} %get-tuple-element.56, f32[256]{0:T(256)S(1)} %get-tuple-element.57, f32[256]{0:T(256)S(1)} %get-tuple-element.58, f32[]{:T(128)} %bitcast.16, f32[]{:T(128)} %bitcast.15, ...), kind=kOutput, calls=%fused_computation.18 | convolution fusion | flops 807010304 | bytes 4463632 | tf_op jit(solution)/shard_map/dot_general | solution.py:28
  52.6 1.6 %reshape.667 = f32[512,1024]{1,0:T(8,128)} reshape(f32[8,256,256]{2,1,0:T(8,128)S(1)} %bitcast.87) | data formatting | bytes 4194304 | tf_op jit(solution)/shard_map/reshape | solution.py:89
  54.2 2.9 %copy.87 = f32[512,1024]{0,1:T(8,128)} copy(f32[512,1024]{1,0:T(8,128)} %reshape.667) | data formatting | bytes 4194304 | tf_op jit(solution)/shard_map/reshape | solution.py:89
  57.2 2.6 %reshape.668 = f32[128,32,128]{2,1,0:T(8,128)} reshape(f32[1024,512]{1,0:T(8,128)} %bitcast.91) | data formatting | bytes 4194304 | tf_op jit(solution)/shard_map/reshape | solution.py:89
  59.8 1.4 %fusion.216 = (f32[]{:T(128)}, f32[]{:T(128)}) fusion(f32[2048,4]{0,1:T(4,128)S(1)} %mul.610, f32[2048,256]{1,0:T(8,128)S(1)} %bitcast.88, s32[256]{0:T(256)S(1)} %get-tuple-element.46), kind=kOutput, calls=%fused_computation.347 | convolution fusion | flops 12608510 | bytes 2130952 | tf_op jit(solution)/shard_map/dot_general | solution.py:28
  61.1 1.2 compare_select_fusion.19
  62.4 1.7 %pad_maximum_fusion = f32[128,33,128]{2,1,0:T(8,128)} fusion(f32[128,1,128]{2,1,0:T(1,128)S(1)} %broadcast_in_dim.14, f32[128,32,128]{2,1,0:T(8,128)S(1)} %copy-done), kind=kLoop, calls=%fused_computation.11 | loop fusion | flops 540672 | bytes 4325376 | tf_op jit(solution)/shard_map/concatenate | solution.py:93
  64.1 6.7 %all-to-all-start.1 = ((f32[128,33,128]{2,1,0:T(8,128)}), f32[128,33,128]{2,1,0:T(8,128)S(1)}, u32[]{:S(2)}, u32[]{:S(2)}) async-start(f32[128,33,128]{2,1,0:T(8,128)} %pad_maximum_fusion), calls=%async_computation.1 | async-start | bytes 5242880 | tf_op jit(solution)/shard_map/all_to_all | solution.py:93
  73.8 1.0 gather_fusion.8
  74.9 1.3 select_add_fusion.9
  76.2 29.5 %all-to-all-done.1 = f32[128,33,128]{2,1,0:T(8,128)S(1)} async-done(((f32[128,33,128]{2,1,0:T(8,128)}), f32[128,33,128]{2,1,0:T(8,128)S(1)}, u32[]{:S(2)}, u32[]{:S(2)}) %all-to-all-start.1) | async-done | bytes 2162720 | tf_op jit(solution)/shard_map/all_to_all | solution.py:93
  105.7 0.8 slice_reduce_fusion
  108.6 1.6 %slice.230 = f32[128,32,128]{2,1,0:T(8,128)} slice(f32[128,33,128]{2,1,0:T(8,128)S(1)} %all-to-all-done.1), slice={[0:128], [0:32], [0:128]} | slice | bytes 4194304 | tf_op jit(solution)/shard_map/slice | solution.py:96
  110.2 4.3 %reshape.673 = f32[32,4,8,8,64]{4,3,2,1,0:T(8,128)} reshape(f32[128,32,128]{2,1,0:T(8,128)} %slice.230) | data formatting | bytes 4194304 | tf_op jit(solution)/shard_map/reshape | solution.py:97
  114.6 8.3 %fusion = f32[4,8,64,256,1]{3,2,4,0,1:T(8,128)S(1)} fusion(f32[32,4,8,8,64]{4,3,2,1,0:T(8,128)} %reshape.673, f32[256]{0:T(256)S(1)} %get-tuple-element.53, f32[256]{0:T(256)S(1)} %get-tuple-element.54, f32[256]{0:T(256)S(1)} %get-tuple-element.55, f32[]{:T(128)} %bitcast.31, s32[256]{0:T(256)S(1)} %get-tuple-element.46, s32[32,8]{1,0:T(8,128)S(1)} %get-tuple-element.62, ...), kind=kOutput, calls=%fused_computation.9 | convolution fusion | flops 806486016 | bytes 4205584 | tf_op jit(solution)/shard_map/dot_general | solution.py:28
  122.9 4.6 %fusion.2 = f32[8,256,256]{2,1,0:T(8,128)S(1)} fusion(f32[4,8,64,256,1]{3,2,4,0,1:T(8,128)S(1)} %fusion, f32[]{:T(128)S(6)} %mul.657, f32[256,256]{1,0:T(8,128)S(1)} %copy.96, f32[8,256]{1,0:T(8,128)S(1)} %copy.94, f32[256]{0:T(256)S(1)} %get-tuple-element.50, f32[256]{0:T(256)S(1)} %get-tuple-element.51, f32[256]{0:T(256)S(1)} %get-tuple-element.52, ...), kind=kOutput, calls=%fused_computation.13 | convolution fusion | flops 808058880 | bytes 4475924 | tf_op jit(solution)/shard_map/dot_general | solution.py:28
  127.4 2.4 %copy.101 = f32[256,2,8,128]{3,1,2,0:T(2,128)} copy(f32[256,2,8,128]{3,2,1,0:T(8,128)S(1)} %bitcast.93) | data formatting | bytes 4194304
  (53 shorter events, 13.4 us)
Async XLA Ops:
  3.7 11.5 %copy-start.1 = (f32[2,16]{1,0:T(2,128)S(1)}, f32[2,16]{1,0:T(2,128)}, u32[]{:S(2)}) copy-start(f32[2,16]{1,0:T(2,128)} %param.3) | copy-start | bytes 388
  3.7 41.1 %all-to-all-start = ((f32[128,2,8,256]{3,2,1,0:T(8,128)}), f32[128,2,8,256]{3,2,1,0:T(8,128)S(1)}, u32[]{:S(2)}, u32[]{:S(2)}) async-start(f32[128,2,8,256]{3,2,1,0:T(8,128)} %copy.82), calls=%async_computation | async-start | bytes 4194304 | tf_op jit(solution)/shard_map/all_to_all | solution.py:68
  59.8 2.6 %copy-start = (f32[128,32,128]{2,1,0:T(8,128)S(1)}, f32[128,32,128]{2,1,0:T(8,128)}, u32[]{:S(2)}) copy-start(f32[128,32,128]{2,1,0:T(8,128)} %reshape.668) | copy-start | bytes 6291460
  64.1 41.6 %all-to-all-start.1 = ((f32[128,33,128]{2,1,0:T(8,128)}), f32[128,33,128]{2,1,0:T(8,128)S(1)}, u32[]{:S(2)}, u32[]{:S(2)}) async-start(f32[128,33,128]{2,1,0:T(8,128)} %pad_maximum_fusion), calls=%async_computation.1 | async-start | bytes 5242880 | tf_op jit(solution)/shard_map/all_to_all | solution.py:93

commit v10 on v5

--- a/solution.py
+++ b/solution.py
@@ -98,13 +98,12 @@
     kernel3 = kernel3.reshape(per, devices // 4, spread).transpose(1, 0, 2)
     current = dot(current, kernel3, (0, 3), (0, 1), BLOCK_PRECISION)
     pattern3 = bond3[jnp.arange(8) % 4][:, column // quarter]
-    current = current * pattern3[None, :, None, :]
     current = dot(current, kernel4.reshape(4, quarter, spread), (0, 2), (0, 1), BLOCK_PRECISION)
     pattern4 = bond4[column % 4][:, column // quarter]
 
     middle_mean = middle_total / whole_count
     last_mean = final_total / middle_mean / whole_count
-    current = current * pattern4[None, :, :] / (middle_mean * last_mean)
+    current = current * (pattern3[:, :, None] * pattern4[None, :, :]) / (middle_mean * last_mean)
     growth = jnp.log(middle_mean) + jnp.log(last_mean)
     return (current.reshape(-1), growth)
 

time: 132 us -> 132 us (level)
  no operation moved by 1% of the time
where the time goes in v10:
time: 132 us
  waiting for transfers between devices  32.6 us (25%)
  local copies, waits for them, and re-layouts  31 us (23%)
  matrix products  24.5 us (19%)
  other arithmetic  21.1 us (16%)
  starting transfers between devices  18.2 us (14%)
  between operations  4.24 us (3%)
    all_to_all x1, waiting for transfers between devices, shards(): lax.all_to_all(jnp.concatenate([sending, extra], axis=1), AXES, 0, 0, til...  29.5 us
    dot_general x7, matrix products, dot(): lax.dot_general(lhs, rhs, ((lhs_dims, rhs_dims), ((), ())), precision=pre...  24.5 us
    all_to_all x1, starting transfers between devices, shards(): received = lax.all_to_all(sending, AXES, 0, 0, tiled=True)  11.5 us
    add x8, other arithmetic, block_kernel(): kernel = kernel * (1.0 + horizontal[level] * chained)[None, :]  9.62 us
    reshape x3, local copies, waits for them, and re-layouts, shards(): sending = current.reshape(per * quarter, -1).T.reshape(devices, -1, LANES)  7.17 us
    all_to_all x1, starting transfers between devices, shards(): lax.all_to_all(jnp.concatenate([sending, extra], axis=1), AXES, 0, 0, til...  6.71 us
    reshape x1, local copies, waits for them, and re-layouts, shards(): current = received.reshape(devices // 4, 4, 8, per, quarter)  4.35 us
    transpose x1, local copies, waits for them, and re-layouts, shards(): sending = jnp.transpose(state.reshape(2, spread, -1, LANES), (3, 0, 2, 1))  3.11 us
  transfers between devices with their start and end apart: 2, of which 2 were waited for; matrix products, arithmetic and copies ran while one was open for 24% of the time, Pallas kernels for 0%

profile of v10, /device:TPU:1, one launch (start us, length us, event | category | flops | bytes accessed | tf_op | source)
XLA Modules:
  0.0 131.6 jit_solution(14930033980035679153)
XLA Ops:
  0.6 3.1 %copy.82 = f32[128,2,8,256]{3,2,1,0:T(8,128)} copy(f32[128,2,8,256]{0,2,3,1:T(8,128)} %bitcast.92) | data formatting | bytes 4194304 | tf_op jit(solution)/shard_map/transpose | solution.py:67
  3.7 11.5 %all-to-all-start = ((f32[128,2,8,256]{3,2,1,0:T(8,128)}), f32[128,2,8,256]{3,2,1,0:T(8,128)S(1)}, u32[]{:S(2)}, u32[]{:S(2)}) async-start(f32[128,2,8,256]{3,2,1,0:T(8,128)} %copy.82), calls=%async_computation | async-start | bytes 4194304 | tf_op jit(solution)/shard_map/all_to_all | solution.py:68
  18.1 1.3 select_add_fusion.3
  19.4 2.8 %multiply_reduce_fusion = f32[256,4]{0,1:T(4,128)S(1)} fusion(f32[4,64]{1,0:T(4,128)S(1)} %get-tuple-element.44, f32[4,64]{1,0:T(4,128)S(1)} %get-tuple-element.45, f32[4,64]{1,0:T(4,128)S(1)} %select_add_fusion.5, f32[]{:T(128)} %bitcast.41, s32[4,64]{1,0:T(4,128)S(1)} %get-tuple-element.40, s32[256]{0:T(256)S(1)} %get-tuple-element.46, f32[]{:T(128)} %bitcast.40, ...), kind=kLoop, calls=%fused_computation.82 | loop fusion | flops 1244160 | bytes 15376 | tf_op jit(solution)/shard_map/reduce_sum | solution.py:76
  23.0 1.0 gather_fusion.4
  25.6 1.4 %select_add_fusion.11 = (f32[256]{0:T(256)S(1)}, f32[256]{0:T(256)S(1)}) fusion(f32[]{:T(128)} %bitcast.42, f32[]{:T(128)} %bitcast.34), kind=kLoop, calls=%fused_computation.319 | loop fusion | flops 16128 | bytes 2056 | tf_op jit(solution)/shard_map/add | solution.py:21
  27.0 1.4 %select_add_fusion.13 = (f32[256]{0:T(256)S(1)}, f32[256]{0:T(256)S(1)}) fusion(f32[]{:T(128)} %bitcast.33, f32[]{:T(128)} %bitcast.32), kind=kLoop, calls=%fused_computation.321 | loop fusion | flops 15104 | bytes 2056 | tf_op jit(solution)/shard_map/add | solution.py:21
  29.2 1.0 gather_fusion.2
  32.9 1.1 fusion.42
  35.7 2.4 %gather_fusion = f32[256]{0:T(256)S(1)} fusion(f32[4,4]{1,0:T(4,128)S(1)} %select_add_fusion.8, s32[256]{0:T(256)S(1)} %bitcast.89), kind=kCustom, calls=%fused_computation | custom fusion | bytes 4096 | tf_op jit(solution)/shard_map/gather | solution.py:69
  38.1 1.1 select_add_fusion.17
  39.2 1.3 select_add_fusion.19
  40.5 1.2 select_add_fusion.15
  41.7 3.1 %all-to-all-done = f32[128,2,8,256]{3,2,1,0:T(8,128)S(1)} async-done(((f32[128,2,8,256]{3,2,1,0:T(8,128)}), f32[128,2,8,256]{3,2,1,0:T(8,128)S(1)}, u32[]{:S(2)}, u32[]{:S(2)}) %all-to-all-start) | async-done | bytes 2097184 | tf_op jit(solution)/shard_map/all_to_all | solution.py:68
  44.8 4.2 %fusion.5 = f32[256,8,256]{2,0,1:T(8,128)S(1)} fusion(f32[256,8,256]{2,1,0:T(8,128)S(1)} %bitcast.90, f32[256]{0:T(256)S(1)} %gather_fusion, f32[256]{0:T(256)S(1)} %get-tuple-element.59, f32[256]{0:T(256)S(1)} %get-tuple-element.60, f32[256]{0:T(256)S(1)} %get-tuple-element.61, f32[]{:T(128)} %bitcast.3, s32[256]{0:T(256)S(1)} %get-tuple-element.46, ...), kind=kOutput, calls=%fused_computation.16 | convolution fusion | flops 806551552 | bytes 4202512 | tf_op jit(solution)/shard_map/dot_general | solution.py:28
  49.0 3.6 %convolution_multiply_fusion = f32[256,8,256]{2,0,1:T(8,128)S(1)} fusion(f32[256,8,256]{2,0,1:T(8,128)S(1)} %fusion.5, f32[256,256]{1,0:T(8,128)S(1)} %copy.86, f32[256]{0:T(256)S(1)} %get-tuple-element.56, f32[256]{0:T(256)S(1)} %get-tuple-element.57, f32[256]{0:T(256)S(1)} %get-tuple-element.58, f32[]{:T(128)} %bitcast.16, f32[]{:T(128)} %bitcast.15, ...), kind=kOutput, calls=%fused_computation.18 | convolution fusion | flops 807010304 | bytes 4463632 | tf_op jit(solution)/shard_map/dot_general | solution.py:28
  52.6 1.6 %reshape.667 = f32[512,1024]{1,0:T(8,128)} reshape(f32[8,256,256]{2,1,0:T(8,128)S(1)} %bitcast.87) | data formatting | bytes 4194304 | tf_op jit(solution)/shard_map/reshape | solution.py:89
  54.2 2.9 %copy.87 = f32[512,1024]{0,1:T(8,128)} copy(f32[512,1024]{1,0:T(8,128)} %reshape.667) | data formatting | bytes 4194304 | tf_op jit(solution)/shard_map/reshape | solution.py:89
  57.2 2.6 %reshape.668 = f32[128,32,128]{2,1,0:T(8,128)} reshape(f32[1024,512]{1,0:T(8,128)} %bitcast.91) | data formatting | bytes 4194304 | tf_op jit(solution)/shard_map/reshape | solution.py:89
  59.8 1.7 %fusion.218 = (f32[]{:T(128)}, f32[]{:T(128)}) fusion(f32[2048,4]{0,1:T(4,128)S(1)} %mul.610, f32[2048,256]{1,0:T(8,128)S(1)} %bitcast.88, s32[256]{0:T(256)S(1)} %get-tuple-element.46), kind=kOutput, calls=%fused_computation.346 | convolution fusion | flops 25191422 | bytes 2130952 | tf_op jit(solution)/shard_map/dot_general | solution.py:28
  61.5 1.2 compare_select_fusion.19
  62.8 1.7 %pad_maximum_fusion = f32[128,33,128]{2,1,0:T(8,128)} fusion(f32[128,1,128]{2,1,0:T(1,128)S(1)} %broadcast_in_dim.14, f32[128,32,128]{2,1,0:T(8,128)S(1)} %copy-done), kind=kLoop, calls=%fused_computation.11 | loop fusion | flops 540672 | bytes 4325376 | tf_op jit(solution)/shard_map/concatenate | solution.py:93
  64.5 6.7 %all-to-all-start.1 = ((f32[128,33,128]{2,1,0:T(8,128)}), f32[128,33,128]{2,1,0:T(8,128)S(1)}, u32[]{:S(2)}, u32[]{:S(2)}) async-start(f32[128,33,128]{2,1,0:T(8,128)} %pad_maximum_fusion), calls=%async_computation.1 | async-start | bytes 5242880 | tf_op jit(solution)/shard_map/all_to_all | solution.py:93
  74.1 1.0 gather_fusion.8
  75.2 1.3 select_add_fusion.9
  76.6 29.5 %all-to-all-done.1 = f32[128,33,128]{2,1,0:T(8,128)S(1)} async-done(((f32[128,33,128]{2,1,0:T(8,128)}), f32[128,33,128]{2,1,0:T(8,128)S(1)}, u32[]{:S(2)}, u32[]{:S(2)}) %all-to-all-start.1) | async-done | bytes 2162720 | tf_op jit(solution)/shard_map/all_to_all | solution.py:93
  106.1 0.8 slice_reduce_fusion
  108.9 1.6 %slice.230 = f32[128,32,128]{2,1,0:T(8,128)} slice(f32[128,33,128]{2,1,0:T(8,128)S(1)} %all-to-all-done.1), slice={[0:128], [0:32], [0:128]} | slice | bytes 4194304 | tf_op jit(solution)/shard_map/slice | solution.py:96
  110.6 4.3 %reshape.673 = f32[32,4,8,8,64]{4,3,2,1,0:T(8,128)} reshape(f32[128,32,128]{2,1,0:T(8,128)} %slice.230) | data formatting | bytes 4194304 | tf_op jit(solution)/shard_map/reshape | solution.py:97
  114.9 8.3 %fusion = f32[4,8,64,256,1]{3,2,4,0,1:T(8,128)S(1)} fusion(f32[32,4,8,8,64]{4,3,2,1,0:T(8,128)} %reshape.673, f32[256]{0:T(256)S(1)} %get-tuple-element.53, f32[256]{0:T(256)S(1)} %get-tuple-element.54, f32[256]{0:T(256)S(1)} %get-tuple-element.55, f32[]{:T(128)} %bitcast.31, s32[256]{0:T(256)S(1)} %get-tuple-element.46, s32[32,8]{1,0:T(8,128)S(1)} %get-tuple-element.62, ...), kind=kOutput, calls=%fused_computation.9 | convolution fusion | flops 806486016 | bytes 4205584 | tf_op jit(solution)/shard_map/dot_general | solution.py:28
  123.2 4.9 %fusion.2 = f32[8,256,256]{2,1,0:T(8,128)S(1)} fusion(f32[4,8,64,256,1]{3,2,4,0,1:T(8,128)S(1)} %fusion, f32[]{:T(128)S(6)} %mul.657, f32[256,256]{1,0:T(8,128)S(1)} %copy.96, f32[8,256]{1,0:T(8,128)S(1)} %copy.94, f32[256]{0:T(256)S(1)} %get-tuple-element.50, f32[256]{0:T(256)S(1)} %get-tuple-element.51, f32[256]{0:T(256)S(1)} %get-tuple-element.52, ...), kind=kOutput, calls=%fused_computation.13 | convolution fusion | flops 808058880 | bytes 4475924 | tf_op jit(solution)/shard_map/dot_general | solution.py:28
  128.1 2.4 %copy.101 = f32[256,2,8,128]{3,1,2,0:T(2,128)} copy(f32[256,2,8,128]{3,2,1,0:T(8,128)S(1)} %bitcast.93) | data formatting | bytes 4194304
  (53 shorter events, 13.4 us)
Async XLA Ops:
  3.7 11.5 %copy-start.1 = (f32[2,16]{1,0:T(2,128)S(1)}, f32[2,16]{1,0:T(2,128)}, u32[]{:S(2)}) copy-start(f32[2,16]{1,0:T(2,128)} %param.3) | copy-start | bytes 388
  3.7 41.1 %all-to-all-start = ((f32[128,2,8,256]{3,2,1,0:T(8,128)}), f32[128,2,8,256]{3,2,1,0:T(8,128)S(1)}, u32[]{:S(2)}, u32[]{:S(2)}) async-start(f32[128,2,8,256]{3,2,1,0:T(8,128)} %copy.82), calls=%async_computation | async-start | bytes 4194304 | tf_op jit(solution)/shard_map/all_to_all | solution.py:68
  59.8 3.0 %copy-start = (f32[128,32,128]{2,1,0:T(8,128)S(1)}, f32[128,32,128]{2,1,0:T(8,128)}, u32[]{:S(2)}) copy-start(f32[128,32,128]{2,1,0:T(8,128)} %reshape.668) | copy-start | bytes 6291460
  64.5 41.6 %all-to-all-start.1 = ((f32[128,33,128]{2,1,0:T(8,128)}), f32[128,33,128]{2,1,0:T(8,128)S(1)}, u32[]{:S(2)}, u32[]{:S(2)}) async-start(f32[128,33,128]{2,1,0:T(8,128)} %pad_maximum_fusion), calls=%async_computation.1 | async-start | bytes 5242880 | tf_op jit(solution)/shard_map/all_to_all | solution.py:93
